TPU v7x, 256 devices: a whole 4x4x8 slice. The times are simulated.
256 devices in a mesh: rect: 64 (over z, x, core), split: 4 (over y).
Axes of the slice: x: 4, y: 4, z: 8, core: 2. Of those that a mesh axis runs over, the one named last changes fastest.
Arguments:
- small_now: float32 [512, 16, 16, 384], P(('rect', 'split')), may hold values from -6 to 6
- small_prev: float32 [512, 16, 16, 384], P(('rect', 'split')), may hold values from -6 to 6
- plaza_now: float32 [64, 64, 16, 384], P('rect', 'split'), may hold values from -6 to 6
- plaza_prev: float32 [64, 64, 16, 384], P('rect', 'split'), may hold values from -6 to 6
- face_partner: int32 [64, 4, 96], P('rect', 'split'), may hold values from -1 to 6143, as said below
Outputs:
- small_modes: float32 [512, 16, 16, 384], P(('rect', 'split'))
- small_before: float32 [512, 16, 16, 384], P(('rect', 'split'))
- plaza_modes: float32 [64, 64, 16, 384], P('rect', 'split')
- plaza_before: float32 [64, 64, 16, 384], P('rect', 'split')
Inputs may be any that keep to these rules, and one draw needn't show every extreme that they name: `face_partner`: an entry of group (r, s) is -1 or r2 * 96 + e2, segment e2 of group (r2, s) with the same s and r2 != r, of the same piece number. Pairing is symmetric; side 1 pairs with side 0 and side 3 with side 2. Every segment is paired except those of sides 0 and 1 of block 2, which are -1. At most 2 segments of one group pair with segments of any one group, and exactly 2 in some pair of groups.
All inputs are finite; a program needn't handle non-finite values.
Results may differ from a plain program's by a relative error of at most 0.0001.
Values sent between devices are 32-bit elements; how exact they have to be, the bound alone decides.
No kernel may reach another device: no remote copies, remote signals or barrier semaphores. Data moves between devices by JAX's collectives and lax.ppermute only.
A program may use at most 64 MiB of HBM per device.

v0:
```python
import jax
import jax.numpy as jnp
from jax import lax
from jax.sharding import PartitionSpec as P

STEPS = 2
COURANT = 0.5
highest = lax.Precision.HIGHEST


def dct_rows_cols(wavenumber, position, length):
    wavenumber = wavenumber.astype(jnp.float32)[:, None]
    position = position.astype(jnp.float32)[None, :]
    weight = jnp.where(wavenumber == 0.0, jnp.sqrt(1.0 / length), jnp.sqrt(2.0 / length))
    return weight * jnp.cos(jnp.pi * wavenumber * (position + 0.5) / length)


def dct_table(length):
    return dct_rows_cols(jnp.arange(length), jnp.arange(length), length)


def update_factors(first_row, row_count, length_x, edge_cells, height_cells):
    wave_x = (first_row + jnp.arange(row_count)).astype(jnp.float32)[:, None, None] / length_x
    wave_y = jnp.arange(edge_cells, dtype=jnp.float32)[None, :, None] / edge_cells
    wave_z = jnp.arange(height_cells, dtype=jnp.float32)[None, None, :] / height_cells
    phase_angle = COURANT * jnp.pi * jnp.sqrt(wave_x**2 + wave_y**2 + wave_z**2)
    twice_cos = 2.0 * jnp.cos(phase_angle)
    forcing_gain = COURANT**2 * jnp.sinc(phase_angle / (2.0 * jnp.pi)) ** 2
    return (twice_cos, forcing_gain)


def interface_layers(difference):
    nearest = difference[:, 0]
    middle = difference[:, 1]
    farthest = difference[:, 2]
    return jnp.stack(
        [
            (270.0 * nearest - 27.0 * middle + 2.0 * farthest) / 180.0,
            (-27.0 * nearest + 2.0 * middle) / 180.0,
            2.0 * nearest / 180.0,
        ],
        axis=1,
    )


def ein(spec, a, b):
    return jnp.einsum(spec, a, b, precision=highest, preferred_element_type=jnp.float32)


def gather_slabs(block):
    count = lax.axis_size("split")
    pieces = [block]
    for shift in range(1, count):
        perm = [(j, (j - shift) % count) for j in range(count)]
        pieces.append(lax.ppermute(block, "split", perm))
    return jnp.concatenate(pieces, axis=0)


def on_device(small_now, small_prev, plaza_now, plaza_prev, face_partner):
    owned = small_now.shape[0]
    edge = small_now.shape[1]
    height = small_now.shape[3]
    slabs = lax.axis_size("split")
    groups = lax.axis_size("rect")
    plaza_len = edge * slabs
    first_row = lax.axis_index("split") * edge

    table_side = dct_table(edge)
    table_height = dct_table(height)
    edge_pos = jnp.array([0, 1, 2, edge - 1, edge - 2, edge - 3], jnp.int32)
    side6 = table_side[:, edge_pos]
    mine = first_row + jnp.arange(edge)
    slab_of = (lax.axis_index("split") + jnp.arange(slabs)) % slabs
    gathered_rows = (slab_of[:, None] * edge + jnp.arange(edge)[None, :]).reshape(-1)
    plaza_cols = dct_rows_cols(gathered_rows, mine, plaza_len)
    plaza_rows = dct_rows_cols(mine, gathered_rows, plaza_len)

    small_cos, small_gain = update_factors(0, edge, edge, edge, height)
    plaza_cos, plaza_gain = update_factors(first_row, edge, plaza_len, edge, height)

    partners = face_partner.reshape(-1)
    seg_count = partners.shape[0]
    face_count = 4 * (owned + 1)
    pieces = seg_count // face_count
    seg_cells = edge // pieces
    unit_count = (2 * owned + 1) * pieces
    slot_most = (unit_count + groups // 2 - 2) // (groups // 2 - 1)
    slots = groups * slot_most
    paired = partners >= 0
    partner_id = jnp.where(paired, partners, 0)
    other_group = partner_id // seg_count
    other_seg = partner_id % seg_count
    same_group = (other_group[:, None] == other_group[None, :]) & paired[:, None] & paired[None, :]
    send_rank = jnp.sum(same_group & (other_seg[None, :] < other_seg[:, None]), axis=1)
    seg_order = jnp.arange(seg_count)
    recv_rank = jnp.sum(same_group & (seg_order[None, :] < seg_order[:, None]), axis=1)
    target = jnp.where(paired, other_group * slot_most + send_rank, -1)
    source = jnp.where(paired, other_group * slot_most + recv_rank, -1)
    slot_ids = jnp.arange(slots)
    send_hot = (slot_ids[:, None] == target[None, :]).astype(jnp.float32)
    send_hot = send_hot.reshape(slots, face_count, pieces)
    recv_hot = (source[:, None] == slot_ids[None, :]).astype(jnp.float32)
    recv_hot = recv_hot.reshape(face_count, pieces, slots)
    pair_mask = paired.reshape(face_count, 1, pieces, 1, 1)

    x_rows = side6[:, None, :, None] * table_side[None, :, None, :]
    y_rows = table_side[:, None, None, :] * side6[None, :, :, None]
    face_rows = jnp.concatenate(
        [x_rows.reshape(edge * edge, 6 * edge), y_rows.reshape(edge * edge, 6 * edge)], axis=1
    )

    def time_step(_, state):
        small_old, small_cur, plaza_old, plaza_cur = state
        flat_modes = small_cur.reshape(owned, edge * edge, height)
        small_strips = ein("rz,zk->rk", ein("pr,bpk->brk", face_rows, flat_modes).reshape(-1, height), table_height)
        small_strips = small_strips.reshape(owned * 4, 3, edge, height)
        plaza_y = ein("iyk,kz->iyz", ein("ijk,jy->iyk", plaza_cur, side6), table_height)
        plaza_all = gather_slabs(plaza_y.reshape(edge, -1))
        plaza_all = plaza_all.reshape(plaza_len, 6, height)
        plaza_faces = ein("iyz,ix->yxz", plaza_all, plaza_cols)
        plaza_strips = jnp.concatenate(
            [jnp.zeros_like(plaza_faces), plaza_faces], axis=0
        ).reshape(4, 3, edge, height)
        strips = jnp.concatenate([small_strips, plaza_strips], axis=0)
        segments = strips.reshape(face_count, 3, pieces, seg_cells, height)
        outgoing = ein("sfq,fmqcz->smcz", send_hot, segments)
        arrived = lax.all_to_all(outgoing, "rect", 0, 0, tiled=True)
        remote = ein("fqs,smcz->fmqcz", recv_hot, arrived)
        difference = jnp.where(pair_mask, remote - segments, 0.0)
        layers = interface_layers(difference.reshape(face_count, 3, edge, height))
        small_layers = ein("rz,kz->rk", layers[: owned * 4].reshape(-1, height), table_height)
        small_force = ein("pr,brk->bpk", face_rows, small_layers.reshape(owned, -1, height))
        small_force = small_force.reshape(owned, edge, edge, height)
        plaza_layers = ein("fmxz,kz->xfmk", layers[owned * 4 + 2 :], table_height)
        plaza_gathered = gather_slabs(plaza_layers.reshape(edge, -1))
        plaza_gathered = plaza_gathered.reshape(plaza_len, 6, height)
        plaza_x = ein("xyk,ix->iyk", plaza_gathered, plaza_rows)
        plaza_force = ein("iyk,jy->ijk", plaza_x, side6)
        small_next = small_cos * small_cur - small_old + small_gain * small_force
        plaza_next = plaza_cos * plaza_cur - plaza_old + plaza_gain * plaza_force
        return (small_cur, small_next, plaza_cur, plaza_next)

    small_old, small_cur, plaza_old, plaza_cur = lax.fori_loop(
        0, STEPS, time_step, (small_prev, small_now, plaza_prev[0], plaza_now[0])
    )
    return (small_cur, small_old, plaza_cur[None], plaza_old[None])


def solution(mesh):
    return jax.shard_map(
        on_device,
        mesh=mesh,
        in_specs=(
            P(("rect", "split"), None, None, None),
            P(("rect", "split"), None, None, None),
            P("rect", "split", None, None),
            P("rect", "split", None, None),
            P("rect", "split", None),
        ),
        out_specs=(
            P(("rect", "split"), None, None, None),
            P(("rect", "split"), None, None, None),
            P("rect", "split", None, None),
            P("rect", "split", None, None),
        ),
        check_vma=False,
    )
```

profile of v0, /device:TPU:2, one launch (start us, length us, event | category | flops | bytes accessed | tf_op | source)
XLA Modules:
  0.0 171.3 jit_solution(3234247539617952735)
XLA Ops:
  0.7 1.1 copy-done.11
  3.5 2.1 %fusion.129 = (f32[16,16,384]{2,1,0:T(8,128)}, f32[16,16,384]{2,1,0:T(8,128)}) fusion(f32[16,16]{1,0:T(8,128)S(1)} %get-tuple-element.746, f32[384]{0:T(512)S(1)} %get-tuple-element.736, f32[16,16]{1,0:T(8,128)S(1)} %get-tuple-element.737), kind=kLoop, calls=%fused_computation.164 | loop fusion | flops 7274496 | bytes 790016 | tf_op jit(solution)/shard_map/mul | solution.py:28
  9.4 160.9 %while.21 = (s32[]{:T(128)}, f32[2,16,16,384]{3,2,1,0:T(8,128)}, f32[2,16,16,384]{3,2,1,0:T(8,128)S(1)}, f32[16,16,384]{2,1,0:T(8,128)}, f32[16,16,384]{2,1,0:T(...) while((s32[]{:T(128)}, f32[2,16,16,384]{3,2,1,0:T(8,128)}, ...), condition=%wide.region_3.5_spmd.clone.clone.clone, body=%wide.region_2.4_spmd.clone.clone.clone.sunk | while | flops 3361830912 | bytes 56945052 | solution.py:143
  9.9 2.6 %fusion.203 = f32[16,6,384]{2,0,1:T(8,128)S(1)} fusion(f32[384]{0:T(512)S(1)} %get-tuple-element.790, f32[384]{0:T(512)S(1)} %get-tuple-element.791, f32[384]{0:T(512)S(1)} %get-tuple-element.792, f32[16,6,384]{2,1,0:T(8,128)S(1)} %convolution_bitcast_fusion.12), kind=kOutput, calls=%fused_computation.50.clone.1 | convolution fusion | flops 170311680 | bytes 299520 | tf_op jit(solution)/shard_map/while/body/eval_jaxpr/iyk,kz->iyz/dot_general | solution.py:47
  12.5 1.7 collective-permute-start
  14.2 2.9 %collective-permute-start.1 = (f32[16,2304]{1,0:T(8,128)S(1)}, f32[16,2304]{1,0:T(8,128)}, u32[]{:S(2)}, u32[]{:S(2)}) collective-permute-start(f32[16,2304]{1,0:T(8,128)S(1)} %bitcast.231), channel_id=1, source_target_pairs={{0,2},{1,3},{2,0},{3,1},{4,6},{5,7},{6,4},{7,5},{8,10},{9,11},{10,... | collective-permute-start | bytes 442376 | tf_op jit(solution)/shard_map/while/body/eval_jaxpr/ppermute | solution.py:55
  17.1 1.3 collective-permute-start.2
  19.5 3.3 %fusion.204 = f32[8,3,8,2,384]{4,2,3,1,0:T(8,128)S(1)} fusion(f32[8,3,8,2,384]{4,3,2,1,0:T(2,128)S(1)} %dot_general.108, f32[384]{0:T(512)S(1)} %get-tuple-element.790, f32[384]{0:T(512)S(1)} %get-tuple-element.791, f32[384]{0:T(512)S(1)} %get-tuple-element.792), kind=kOutput, calls=%fused_computation.46.clone.1 | convolution fusion | flops 679919616 | bytes 1184256 | tf_op jit(solution)/shard_map/while/body/eval_jaxpr/rz,zk->rk/dot_general | solution.py:47
  26.5 2.1 %convolution_bitcast_fusion.15 = f32[128,3,2,384]{0,3,1,2:T(8,128)S(1)} fusion(s32[12,8]{1,0:T(8,128)S(1)} %get-tuple-element.796, f32[4,3,8,2,384]{4,2,3,1,0:T(8,128)S(1)} %copy.131, f32[8,3,8,2,384]{4,2,3,1,0:T(8,128)S(1)} %fusion.204), kind=kOutput, calls=%fused_computation.8.clone.1 | convolution fusion | flops 339984384 | bytes 2064768 | tf_op jit(solution)/shard_map/while/body/eval_jaxpr/sfq,fmqcz->smcz/dot_general | solution.py:47
  28.6 2.0 %copy.132 = f32[128,3,2,384]{3,2,1,0:T(2,128)} copy(f32[128,3,2,384]{0,3,1,2:T(8,128)S(1)} %convolution_bitcast_fusion.15) | data formatting | bytes 2359296 | tf_op jit(solution)/shard_map/while/body/eval_jaxpr/sfq,fmqcz->smcz/dot_general | solution.py:47
  30.6 12.0 %all-to-all-start = ((f32[128,3,2,384]{3,2,1,0:T(2,128)}), f32[128,3,2,384]{3,2,1,0:T(2,128)S(1)}, u32[]{:S(2)}, u32[]{:S(2)}) async-start(f32[128,3,2,384]{3,2,1,0:T(2,128)} %copy.132), calls=%async_computation | async-start | bytes 2359296 | tf_op jit(solution)/shard_map/while/body/eval_jaxpr/all_to_all | solution.py:127
  42.7 2.2 %cosine_multiply_fusion.8 = f32[16,16,384]{2,1,0:T(8,128)} fusion(f32[384]{0:T(512)S(1)} %get-tuple-element.788, f32[16,16]{1,0:T(8,128)S(1)} %get-tuple-element.789), kind=kLoop, calls=%fused_computation.56.clone.1 | loop fusion | flops 294912 | bytes 395776 | tf_op jit(solution)/shard_map/mul | solution.py:27
  44.9 29.3 %all-to-all-done = f32[128,3,2,384]{3,2,1,0:T(2,128)S(1)} async-done(((f32[128,3,2,384]{3,2,1,0:T(2,128)}), f32[128,3,2,384]{3,2,1,0:T(2,128)S(1)}, u32[]{:S(2)}, u32[]{:S(2)}) %all-to-all-start) | async-done | bytes 1179680 | tf_op jit(solution)/shard_map/while/body/eval_jaxpr/all_to_all | solution.py:127
  76.4 2.8 %fusion.209 = f32[2,3,16,384]{3,2,1,0:T(8,128)S(1)} fusion(f32[12,1,16,384]{3,2,1,0:T(8,128)S(1)} %get-tuple-element.723, f32[12,1,16,384]{3,2,1,0:T(8,128)S(1)} %get-tuple-element.724, f32[12,1,16,384]{3,2,1,0:T(8,128)S(1)} %get-tuple-element.725, f32[384]{0:T(512)S(1)} %get-tuple-element.790, f32[384]{0:T(512)S(1)} %get-tuple-element.791, ...), kind=kOutput, calls=%fused_computation.22.clone.1 | convolution fusion | flops 170754048 | bytes 1036800 | tf_op jit(solution)/shard_map/while/body/eval_jaxpr/fmxz,kz->xfmk/dot_general | solution.py:47
  80.5 2.1 %collective-permute-start.4 = (f32[16,2304]{1,0:T(8,128)}, f32[16,2304]{1,0:T(8,128)S(1)}, u32[]{:S(2)}, u32[]{:S(2)}) collective-permute-start(f32[16,2304]{1,0:T(8,128)} %reshape.570), channel_id=1, source_target_pairs={{0,2},{1,3},{2,0},{3,1},{4,6},{5,7},{6,4},{7,5},{8,10},{9,11},{10,... | collective-permute-start | bytes 442376 | tf_op jit(solution)/shard_map/while/body/eval_jaxpr/ppermute | solution.py:55
  82.7 1.6 collective-permute-start.5
  84.4 3.3 %fusion.207 = f32[2,192,384]{2,1,0:T(8,128)S(1)} fusion(f32[2,192,384]{2,1,0:T(8,128)S(1)} %bitcast.221, f32[384]{0:T(512)S(1)} %get-tuple-element.790, f32[384]{0:T(512)S(1)} %get-tuple-element.791, f32[384]{0:T(512)S(1)} %get-tuple-element.792), kind=kOutput, calls=%fused_computation.48.clone.1 | convolution fusion | flops 679919616 | bytes 1184256 | tf_op jit(solution)/shard_map/while/body/eval_jaxpr/rz,kz->rk/dot_general | solution.py:47
  91.1 1.9 %fusion.210 = f32[16,16,384]{2,1,0:T(8,128)S(1)} fusion(f32[16,16,384]{2,1,0:T(8,128)S(1)} %copy-done.8, f32[16,16,384]{2,1,0:T(8,128)S(1)} %copy-done.9, f32[16,16,384]{2,1,0:T(8,128)S(1)} %get-tuple-element.756, f32[16,6,384]{2,0,1:T(8,128)S(1)} %convolution_bitcast_fusion.16, f32[16,16]{1,0:T(8,128)S(1)} %get-tuple-element.798, ...), kind=kOutput, calls=%fused_computation.15.clone.1 | convolution fusion | flops 7766016 | bytes 1723264 | tf_op jit(solution)/shard_map/while/body/eval_jaxpr/iyk,jy->ijk/dot_general | solution.py:47
  94.1 2.6 %fusion.203 = f32[16,6,384]{2,0,1:T(8,128)S(1)} fusion(f32[384]{0:T(512)S(1)} %get-tuple-element.790, f32[384]{0:T(512)S(1)} %get-tuple-element.791, f32[384]{0:T(512)S(1)} %get-tuple-element.792, f32[16,6,384]{2,1,0:T(8,128)S(1)} %convolution_bitcast_fusion.12), kind=kOutput, calls=%fused_computation.50.clone.1 | convolution fusion | flops 170311680 | bytes 299520 | tf_op jit(solution)/shard_map/while/body/eval_jaxpr/iyk,kz->iyz/dot_general | solution.py:47
  97.2 2.8 %collective-permute-start.1 = (f32[16,2304]{1,0:T(8,128)S(1)}, f32[16,2304]{1,0:T(8,128)}, u32[]{:S(2)}, u32[]{:S(2)}) collective-permute-start(f32[16,2304]{1,0:T(8,128)S(1)} %bitcast.231), channel_id=1, source_target_pairs={{0,2},{1,3},{2,0},{3,1},{4,6},{5,7},{6,4},{7,5},{8,10},{9,11},{10,... | collective-permute-start | bytes 442376 | tf_op jit(solution)/shard_map/while/body/eval_jaxpr/ppermute | solution.py:55
  100.0 1.3 collective-permute-start.2
  102.4 3.3 %fusion.204 = f32[8,3,8,2,384]{4,2,3,1,0:T(8,128)S(1)} fusion(f32[8,3,8,2,384]{4,3,2,1,0:T(2,128)S(1)} %dot_general.108, f32[384]{0:T(512)S(1)} %get-tuple-element.790, f32[384]{0:T(512)S(1)} %get-tuple-element.791, f32[384]{0:T(512)S(1)} %get-tuple-element.792), kind=kOutput, calls=%fused_computation.46.clone.1 | convolution fusion | flops 679919616 | bytes 1184256 | tf_op jit(solution)/shard_map/while/body/eval_jaxpr/rz,zk->rk/dot_general | solution.py:47
  109.2 2.1 %convolution_bitcast_fusion.15 = f32[128,3,2,384]{0,3,1,2:T(8,128)S(1)} fusion(s32[12,8]{1,0:T(8,128)S(1)} %get-tuple-element.796, f32[4,3,8,2,384]{4,2,3,1,0:T(8,128)S(1)} %copy.131, f32[8,3,8,2,384]{4,2,3,1,0:T(8,128)S(1)} %fusion.204), kind=kOutput, calls=%fused_computation.8.clone.1 | convolution fusion | flops 339984384 | bytes 2064768 | tf_op jit(solution)/shard_map/while/body/eval_jaxpr/sfq,fmqcz->smcz/dot_general | solution.py:47
  111.3 2.0 %copy.132 = f32[128,3,2,384]{3,2,1,0:T(2,128)} copy(f32[128,3,2,384]{0,3,1,2:T(8,128)S(1)} %convolution_bitcast_fusion.15) | data formatting | bytes 2359296 | tf_op jit(solution)/shard_map/while/body/eval_jaxpr/sfq,fmqcz->smcz/dot_general | solution.py:47
  113.3 6.8 %all-to-all-start = ((f32[128,3,2,384]{3,2,1,0:T(2,128)}), f32[128,3,2,384]{3,2,1,0:T(2,128)S(1)}, u32[]{:S(2)}, u32[]{:S(2)}) async-start(f32[128,3,2,384]{3,2,1,0:T(2,128)} %copy.132), calls=%async_computation | async-start | bytes 2359296 | tf_op jit(solution)/shard_map/while/body/eval_jaxpr/all_to_all | solution.py:127
  120.2 2.2 %cosine_multiply_fusion.8 = f32[16,16,384]{2,1,0:T(8,128)} fusion(f32[384]{0:T(512)S(1)} %get-tuple-element.788, f32[16,16]{1,0:T(8,128)S(1)} %get-tuple-element.789), kind=kLoop, calls=%fused_computation.56.clone.1 | loop fusion | flops 294912 | bytes 395776 | tf_op jit(solution)/shard_map/mul | solution.py:27
  122.4 29.3 %all-to-all-done = f32[128,3,2,384]{3,2,1,0:T(2,128)S(1)} async-done(((f32[128,3,2,384]{3,2,1,0:T(2,128)}), f32[128,3,2,384]{3,2,1,0:T(2,128)S(1)}, u32[]{:S(2)}, u32[]{:S(2)}) %all-to-all-start) | async-done | bytes 1179680 | tf_op jit(solution)/shard_map/while/body/eval_jaxpr/all_to_all | solution.py:127
  151.7 1.0 fusion.205
  153.9 2.8 %fusion.209 = f32[2,3,16,384]{3,2,1,0:T(8,128)S(1)} fusion(f32[12,1,16,384]{3,2,1,0:T(8,128)S(1)} %get-tuple-element.723, f32[12,1,16,384]{3,2,1,0:T(8,128)S(1)} %get-tuple-element.724, f32[12,1,16,384]{3,2,1,0:T(8,128)S(1)} %get-tuple-element.725, f32[384]{0:T(512)S(1)} %get-tuple-element.790, f32[384]{0:T(512)S(1)} %get-tuple-element.791, ...), kind=kOutput, calls=%fused_computation.22.clone.1 | convolution fusion | flops 170754048 | bytes 1036800 | tf_op jit(solution)/shard_map/while/body/eval_jaxpr/fmxz,kz->xfmk/dot_general | solution.py:47
  157.9 2.3 %collective-permute-start.4 = (f32[16,2304]{1,0:T(8,128)}, f32[16,2304]{1,0:T(8,128)S(1)}, u32[]{:S(2)}, u32[]{:S(2)}) collective-permute-start(f32[16,2304]{1,0:T(8,128)} %reshape.570), channel_id=1, source_target_pairs={{0,2},{1,3},{2,0},{3,1},{4,6},{5,7},{6,4},{7,5},{8,10},{9,11},{10,... | collective-permute-start | bytes 442376 | tf_op jit(solution)/shard_map/while/body/eval_jaxpr/ppermute | solution.py:55
  160.8 3.3 %fusion.207 = f32[2,192,384]{2,1,0:T(8,128)S(1)} fusion(f32[2,192,384]{2,1,0:T(8,128)S(1)} %bitcast.221, f32[384]{0:T(512)S(1)} %get-tuple-element.790, f32[384]{0:T(512)S(1)} %get-tuple-element.791, f32[384]{0:T(512)S(1)} %get-tuple-element.792), kind=kOutput, calls=%fused_computation.48.clone.1 | convolution fusion | flops 679919616 | bytes 1184256 | tf_op jit(solution)/shard_map/while/body/eval_jaxpr/rz,kz->rk/dot_general | solution.py:47
  167.7 1.9 %fusion.210 = f32[16,16,384]{2,1,0:T(8,128)S(1)} fusion(f32[16,16,384]{2,1,0:T(8,128)S(1)} %copy-done.8, f32[16,16,384]{2,1,0:T(8,128)S(1)} %copy-done.9, f32[16,16,384]{2,1,0:T(8,128)S(1)} %get-tuple-element.756, f32[16,6,384]{2,0,1:T(8,128)S(1)} %convolution_bitcast_fusion.16, f32[16,16]{1,0:T(8,128)S(1)} %get-tuple-element.798, ...), kind=kOutput, calls=%fused_computation.15.clone.1 | convolution fusion | flops 7766016 | bytes 1723264 | tf_op jit(solution)/shard_map/while/body/eval_jaxpr/iyk,jy->ijk/dot_general | solution.py:47
  (150 shorter events, 31.8 us)
Async XLA Ops:
  0.6 1.1 copy-start.11
  0.6 2.0 %copy-start.12 = (f32[1,16,16,384]{3,2,1,0:T(8,128)S(1)}, f32[1,16,16,384]{3,2,1,0:T(8,128)}, u32[]{:S(2)}) copy-start(f32[1,16,16,384]{3,2,1,0:T(8,128)} %param.12) | copy-start | bytes 1179652
  2.6 3.1 %copy-start.13 = (s32[6]{0:T(128)S(1)}, s32[6]{0:T(128)}, u32[]{:S(2)}) copy-start(s32[6]{0:T(128)} %constant.191) | copy-start | bytes 76
  6.5 2.9 %copy-start.1 = (f32[2,16,16,384]{3,2,1,0:T(8,128)S(1)}, f32[2,16,16,384]{3,2,1,0:T(8,128)}, u32[]{:S(2)}) copy-start(f32[2,16,16,384]{3,2,1,0:T(8,128)} %param.9) | copy-start | bytes 2359300
  6.5 2.9 %copy-start.3 = (f32[1,16,16,384]{3,2,1,0:T(8,128)S(1)}, f32[1,16,16,384]{3,2,1,0:T(8,128)}, u32[]{:S(2)}) copy-start(f32[1,16,16,384]{3,2,1,0:T(8,128)} %param.11) | copy-start | bytes 1179652
  12.5 10.3 %collective-permute-start = (f32[16,2304]{1,0:T(8,128)S(1)}, f32[16,2304]{1,0:T(8,128)}, u32[]{:S(2)}, u32[]{:S(2)}) collective-permute-start(f32[16,2304]{1,0:T(8,128)S(1)} %bitcast.230), channel_id=1, source_target_pairs={{0,1},{1,2},{2,3},{3,0},{4,5},{5,6},{6,7},{7,4},{8,9},{9,10},{10,1... | collective-permute-start | bytes 442376 | tf_op jit(solution)/shard_map/while/body/eval_jaxpr/ppermute | solution.py:55
  14.2 9.7 %collective-permute-start.1 = (f32[16,2304]{1,0:T(8,128)S(1)}, f32[16,2304]{1,0:T(8,128)}, u32[]{:S(2)}, u32[]{:S(2)}) collective-permute-start(f32[16,2304]{1,0:T(8,128)S(1)} %bitcast.231), channel_id=1, source_target_pairs={{0,2},{1,3},{2,0},{3,1},{4,6},{5,7},{6,4},{7,5},{8,10},{9,11},{10,... | collective-permute-start | bytes 442376 | tf_op jit(solution)/shard_map/while/body/eval_jaxpr/ppermute | solution.py:55
  17.1 7.8 %collective-permute-start.2 = (f32[16,2304]{1,0:T(8,128)S(1)}, f32[16,2304]{1,0:T(8,128)}, u32[]{:S(2)}, u32[]{:S(2)}) collective-permute-start(f32[16,2304]{1,0:T(8,128)S(1)} %bitcast.232), channel_id=1, source_target_pairs={{0,3},{1,0},{2,1},{3,2},{4,7},{5,4},{6,5},{7,6},{8,11},{9,8},{10,9... | collective-permute-start | bytes 442376 | tf_op jit(solution)/shard_map/while/body/eval_jaxpr/ppermute | solution.py:55
  30.6 43.6 %all-to-all-start = ((f32[128,3,2,384]{3,2,1,0:T(2,128)}), f32[128,3,2,384]{3,2,1,0:T(2,128)S(1)}, u32[]{:S(2)}, u32[]{:S(2)}) async-start(f32[128,3,2,384]{3,2,1,0:T(2,128)} %copy.132), calls=%async_computation | async-start | bytes 2359296 | tf_op jit(solution)/shard_map/while/body/eval_jaxpr/all_to_all | solution.py:127
  79.2 5.2 %copy-start.6 = (f32[2,3,16,384]{3,2,1,0:T(8,128)}, f32[2,3,16,384]{3,2,1,0:T(8,128)S(1)}, u32[]{:S(2)}) copy-start(f32[2,3,16,384]{3,2,1,0:T(8,128)S(1)} %fusion.209) | copy-start | bytes 442372 | tf_op jit(solution)/shard_map/while
  80.0 9.8 %collective-permute-start.3 = (f32[16,2304]{1,0:T(8,128)}, f32[16,2304]{1,0:T(8,128)S(1)}, u32[]{:S(2)}, u32[]{:S(2)}) collective-permute-start(f32[16,2304]{1,0:T(8,128)} %reshape.570), channel_id=1, source_target_pairs={{0,1},{1,2},{2,3},{3,0},{4,5},{5,6},{6,7},{7,4},{8,9},{9,10},{10,1... | collective-permute-start | bytes 442376 | tf_op jit(solution)/shard_map/while/body/eval_jaxpr/ppermute | solution.py:55
  80.5 9.3 %collective-permute-start.4 = (f32[16,2304]{1,0:T(8,128)}, f32[16,2304]{1,0:T(8,128)S(1)}, u32[]{:S(2)}, u32[]{:S(2)}) collective-permute-start(f32[16,2304]{1,0:T(8,128)} %reshape.570), channel_id=1, source_target_pairs={{0,2},{1,3},{2,0},{3,1},{4,6},{5,7},{6,4},{7,5},{8,10},{9,11},{10,... | collective-permute-start | bytes 442376 | tf_op jit(solution)/shard_map/while/body/eval_jaxpr/ppermute | solution.py:55
  82.7 7.2 %collective-permute-start.5 = (f32[16,2304]{1,0:T(8,128)}, f32[16,2304]{1,0:T(8,128)S(1)}, u32[]{:S(2)}, u32[]{:S(2)}) collective-permute-start(f32[16,2304]{1,0:T(8,128)} %reshape.570), channel_id=1, source_target_pairs={{0,3},{1,0},{2,1},{3,2},{4,7},{5,4},{6,5},{7,6},{8,11},{9,8},{10,9... | collective-permute-start | bytes 442376 | tf_op jit(solution)/shard_map/while/body/eval_jaxpr/ppermute | solution.py:55
  84.3 4.2 %copy-start.4 = (f32[16,16,384]{2,1,0:T(8,128)S(1)}, f32[16,16,384]{2,1,0:T(8,128)}, u32[]{:S(2)}) copy-start(f32[16,16,384]{2,1,0:T(8,128)} %cosine_multiply_fusion.8) | copy-start | bytes 1179652 | tf_op jit(solution)/shard_map/while
  84.4 4.2 %copy-start.5 = (f32[2,16,16,384]{3,2,1,0:T(8,128)S(1)}, f32[2,16,16,384]{3,2,1,0:T(8,128)}, u32[]{:S(2)}) copy-start(f32[2,16,16,384]{3,2,1,0:T(8,128)} %get-tuple-element.753) | copy-start | bytes 2359300 | tf_op jit(solution)/shard_map/while
  84.4 4.2 %copy-start.10 = (f32[16,16,384]{2,1,0:T(8,128)S(1)}, f32[16,16,384]{2,1,0:T(8,128)}, u32[]{:S(2)}) copy-start(f32[16,16,384]{2,1,0:T(8,128)} %get-tuple-element.783) | copy-start | bytes 1179652 | tf_op jit(solution)/shard_map/while
  89.8 1.3 copy-start.8
  89.8 1.3 copy-start.9
  96.7 9.0 %collective-permute-start = (f32[16,2304]{1,0:T(8,128)S(1)}, f32[16,2304]{1,0:T(8,128)}, u32[]{:S(2)}, u32[]{:S(2)}) collective-permute-start(f32[16,2304]{1,0:T(8,128)S(1)} %bitcast.230), channel_id=1, source_target_pairs={{0,1},{1,2},{2,3},{3,0},{4,5},{5,6},{6,7},{7,4},{8,9},{9,10},{10,1... | collective-permute-start | bytes 442376 | tf_op jit(solution)/shard_map/while/body/eval_jaxpr/ppermute | solution.py:55
  97.2 9.4 %collective-permute-start.1 = (f32[16,2304]{1,0:T(8,128)S(1)}, f32[16,2304]{1,0:T(8,128)}, u32[]{:S(2)}, u32[]{:S(2)}) collective-permute-start(f32[16,2304]{1,0:T(8,128)S(1)} %bitcast.231), channel_id=1, source_target_pairs={{0,2},{1,3},{2,0},{3,1},{4,6},{5,7},{6,4},{7,5},{8,10},{9,11},{10,... | collective-permute-start | bytes 442376 | tf_op jit(solution)/shard_map/while/body/eval_jaxpr/ppermute | solution.py:55
  100.0 7.6 %collective-permute-start.2 = (f32[16,2304]{1,0:T(8,128)S(1)}, f32[16,2304]{1,0:T(8,128)}, u32[]{:S(2)}, u32[]{:S(2)}) collective-permute-start(f32[16,2304]{1,0:T(8,128)S(1)} %bitcast.232), channel_id=1, source_target_pairs={{0,3},{1,0},{2,1},{3,2},{4,7},{5,4},{6,5},{7,6},{8,11},{9,8},{10,9... | collective-permute-start | bytes 442376 | tf_op jit(solution)/shard_map/while/body/eval_jaxpr/ppermute | solution.py:55
  113.3 38.4 %all-to-all-start = ((f32[128,3,2,384]{3,2,1,0:T(2,128)}), f32[128,3,2,384]{3,2,1,0:T(2,128)S(1)}, u32[]{:S(2)}, u32[]{:S(2)}) async-start(f32[128,3,2,384]{3,2,1,0:T(2,128)} %copy.132), calls=%async_computation | async-start | bytes 2359296 | tf_op jit(solution)/shard_map/while/body/eval_jaxpr/all_to_all | solution.py:127
  156.6 4.1 %copy-start.6 = (f32[2,3,16,384]{3,2,1,0:T(8,128)}, f32[2,3,16,384]{3,2,1,0:T(8,128)S(1)}, u32[]{:S(2)}) copy-start(f32[2,3,16,384]{3,2,1,0:T(8,128)S(1)} %fusion.209) | copy-start | bytes 442372 | tf_op jit(solution)/shard_map/while
  157.5 9.1 %collective-permute-start.3 = (f32[16,2304]{1,0:T(8,128)}, f32[16,2304]{1,0:T(8,128)S(1)}, u32[]{:S(2)}, u32[]{:S(2)}) collective-permute-start(f32[16,2304]{1,0:T(8,128)} %reshape.570), channel_id=1, source_target_pairs={{0,1},{1,2},{2,3},{3,0},{4,5},{5,6},{6,7},{7,4},{8,9},{9,10},{10,1... | collective-permute-start | bytes 442376 | tf_op jit(solution)/shard_map/while/body/eval_jaxpr/ppermute | solution.py:55
  157.9 8.7 %collective-permute-start.4 = (f32[16,2304]{1,0:T(8,128)}, f32[16,2304]{1,0:T(8,128)S(1)}, u32[]{:S(2)}, u32[]{:S(2)}) collective-permute-start(f32[16,2304]{1,0:T(8,128)} %reshape.570), channel_id=1, source_target_pairs={{0,2},{1,3},{2,0},{3,1},{4,6},{5,7},{6,4},{7,5},{8,10},{9,11},{10,... | collective-permute-start | bytes 442376 | tf_op jit(solution)/shard_map/while/body/eval_jaxpr/ppermute | solution.py:55
  160.2 7.0 %collective-permute-start.5 = (f32[16,2304]{1,0:T(8,128)}, f32[16,2304]{1,0:T(8,128)S(1)}, u32[]{:S(2)}, u32[]{:S(2)}) collective-permute-start(f32[16,2304]{1,0:T(8,128)} %reshape.570), channel_id=1, source_target_pairs={{0,3},{1,0},{2,1},{3,2},{4,7},{5,4},{6,5},{7,6},{8,11},{9,8},{10,9... | collective-permute-start | bytes 442376 | tf_op jit(solution)/shard_map/while/body/eval_jaxpr/ppermute | solution.py:55
  160.8 4.2 %copy-start.4 = (f32[16,16,384]{2,1,0:T(8,128)S(1)}, f32[16,16,384]{2,1,0:T(8,128)}, u32[]{:S(2)}) copy-start(f32[16,16,384]{2,1,0:T(8,128)} %cosine_multiply_fusion.8) | copy-start | bytes 1179652 | tf_op jit(solution)/shard_map/while
  160.8 4.2 %copy-start.5 = (f32[2,16,16,384]{3,2,1,0:T(8,128)S(1)}, f32[2,16,16,384]{3,2,1,0:T(8,128)}, u32[]{:S(2)}) copy-start(f32[2,16,16,384]{3,2,1,0:T(8,128)} %get-tuple-element.753) | copy-start | bytes 2359300 | tf_op jit(solution)/shard_map/while
  160.8 4.2 %copy-start.10 = (f32[16,16,384]{2,1,0:T(8,128)S(1)}, f32[16,16,384]{2,1,0:T(8,128)}, u32[]{:S(2)}) copy-start(f32[16,16,384]{2,1,0:T(8,128)} %get-tuple-element.783) | copy-start | bytes 1179652 | tf_op jit(solution)/shard_map/while
  166.1 1.0 copy-start.7
  166.2 1.5 copy-start.8
  166.2 1.5 copy-start.9
  (4 other events, 3.5 us)
where the time goes:
time: 172 us; the launch traced here: 171 us
  waiting for transfers between devices  59.6 us (35%)
  matrix products  39.6 us (23%)
  starting transfers between devices  36.8 us (21%)
  local copies, waits for them, and re-layouts  25 us (15%)
  other arithmetic  8.66 us (5%)
    all_to_all x2, waiting for transfers between devices, time_step(): arrived = lax.all_to_all(outgoing, 'rect', 0, 0, tiled=True)  58.6 us
    dot_general x24, matrix products, ein(): jnp.einsum(spec, a, b, precision=highest, preferred_element_type=jnp.floa...  39.6 us
    all_to_all x2, starting transfers between devices, time_step(): arrived = lax.all_to_all(outgoing, 'rect', 0, 0, tiled=True)  18.8 us
    ppermute x12, starting transfers between devices, gather_slabs(): pieces.append(lax.ppermute(block, 'split', perm))  18 us
    concatenate x12, local copies, waits for them, and re-layouts, gather_slabs(): return jnp.concatenate(pieces, axis=0)  5.59 us
    dot_general x4, local copies, waits for them, and re-layouts, ein(): jnp.einsum(spec, a, b, precision=highest, preferred_element_type=jnp.floa...  4.65 us
    mul x2, other arithmetic, update_factors(): twice_cos = 2.0 * jnp.cos(phase_angle)  4.45 us
    unnamed x20, local copies, waits for them, and re-layouts  4.39 us
  transfers between devices with their start and end apart: 14, of which 5 were waited for; matrix products, arithmetic and copies ran while one was open for 16% of the time, Pallas kernels for 0%

commit v1 on v0

--- a/solution.py
+++ b/solution.py
@@ -47,13 +47,13 @@
     return jnp.einsum(spec, a, b, precision=highest, preferred_element_type=jnp.float32)
 
 
-def gather_slabs(block):
+def slab_pieces(block):
     count = lax.axis_size("split")
     pieces = [block]
     for shift in range(1, count):
         perm = [(j, (j - shift) % count) for j in range(count)]
         pieces.append(lax.ppermute(block, "split", perm))
-    return jnp.concatenate(pieces, axis=0)
+    return pieces
 
 
 def on_device(small_now, small_prev, plaza_now, plaza_prev, face_partner):
@@ -74,6 +74,8 @@
     gathered_rows = (slab_of[:, None] * edge + jnp.arange(edge)[None, :]).reshape(-1)
     plaza_cols = dct_rows_cols(gathered_rows, mine, plaza_len)
     plaza_rows = dct_rows_cols(mine, gathered_rows, plaza_len)
+    cols_by_slab = [plaza_cols[t * edge : (t + 1) * edge].T for t in range(slabs)]
+    rows_by_slab = [plaza_rows[:, t * edge : (t + 1) * edge] for t in range(slabs)]
 
     small_cos, small_gain = update_factors(0, edge, edge, edge, height)
     plaza_cos, plaza_gain = update_factors(first_row, edge, plaza_len, edge, height)
@@ -115,9 +117,11 @@
         small_strips = ein("rz,zk->rk", ein("pr,bpk->brk", face_rows, flat_modes).reshape(-1, height), table_height)
         small_strips = small_strips.reshape(owned * 4, 3, edge, height)
         plaza_y = ein("iyk,kz->iyz", ein("ijk,jy->iyk", plaza_cur, side6), table_height)
-        plaza_all = gather_slabs(plaza_y.reshape(edge, -1))
-        plaza_all = plaza_all.reshape(plaza_len, 6, height)
-        plaza_faces = ein("iyz,ix->yxz", plaza_all, plaza_cols)
+        plaza_faces = sum(
+            ein("xi,id->xd", cols_by_slab[t], piece)
+            for t, piece in enumerate(slab_pieces(plaza_y.reshape(edge, -1)))
+        )
+        plaza_faces = jnp.swapaxes(plaza_faces.reshape(edge, 6, height), 0, 1)
         plaza_strips = jnp.concatenate(
             [jnp.zeros_like(plaza_faces), plaza_faces], axis=0
         ).reshape(4, 3, edge, height)
@@ -132,9 +136,10 @@
         small_force = ein("pr,brk->bpk", face_rows, small_layers.reshape(owned, -1, height))
         small_force = small_force.reshape(owned, edge, edge, height)
         plaza_layers = ein("fmxz,kz->xfmk", layers[owned * 4 + 2 :], table_height)
-        plaza_gathered = gather_slabs(plaza_layers.reshape(edge, -1))
-        plaza_gathered = plaza_gathered.reshape(plaza_len, 6, height)
-        plaza_x = ein("xyk,ix->iyk", plaza_gathered, plaza_rows)
+        plaza_x = sum(
+            ein("ix,xd->id", rows_by_slab[t], piece)
+            for t, piece in enumerate(slab_pieces(plaza_layers.reshape(edge, -1)))
+        ).reshape(edge, 6, height)
         plaza_force = ein("iyk,jy->ijk", plaza_x, side6)
         small_next = small_cos * small_cur - small_old + small_gain * small_force
         plaza_next = plaza_cos * plaza_cur - plaza_old + plaza_gain * plaza_force

time: 172 us -> 178 us (1.035)
  matrix products: 39.6 us -> 50.7 us
  local copies, waits for them, and re-layouts: 25 us -> 20.8 us
  starting transfers between devices: 36.8 us -> 34.5 us
    dot_general x24 -> x36, matrix products: 39.6 us -> 50.7 us  [ein(): jnp.einsum(spec, a, b, precision=highest, preferred_element_type=jnp.floa...]
    concatenate x12 -> x0, local copies, waits for them, and re-layouts: 5.59 us -> none  [gather_slabs(): return jnp.concatenate(pieces, axis=0)]
  transfers between devices with their start and end apart: 14 -> 14, of which waited for: 5 -> 5; matrix products, arithmetic and copies ran while one was open for 16% -> 19% of each run, Pallas kernels for 0% -> 0%
where the time goes in v1:
time: 178 us; the launch traced here: 177 us
  waiting for transfers between devices  59.5 us (33%)
  matrix products  50.7 us (28%)
  starting transfers between devices  34.5 us (19%)
  local copies, waits for them, and re-layouts  20.8 us (12%)
  other arithmetic  9.58 us (5%)
    all_to_all x2, waiting for transfers between devices, time_step(): arrived = lax.all_to_all(outgoing, 'rect', 0, 0, tiled=True)  57.2 us
    dot_general x36, matrix products, ein(): jnp.einsum(spec, a, b, precision=highest, preferred_element_type=jnp.floa...  50.7 us
    all_to_all x2, starting transfers between devices, time_step(): arrived = lax.all_to_all(outgoing, 'rect', 0, 0, tiled=True)  17.9 us
    ppermute x12, starting transfers between devices, slab_pieces(): pieces.append(lax.ppermute(block, 'split', perm))  16.5 us
    dot_general x4, local copies, waits for them, and re-layouts, ein(): jnp.einsum(spec, a, b, precision=highest, preferred_element_type=jnp.floa...  4.72 us
    unnamed x20, local copies, waits for them, and re-layouts  4.47 us
    mul x2, other arithmetic, update_factors(): twice_cos = 2.0 * jnp.cos(phase_angle)  4.42 us
  transfers between devices with their start and end apart: 14, of which 5 were waited for; matrix products, arithmetic and copies ran while one was open for 19% of the time, Pallas kernels for 0%

profile of v1, /device:TPU:2, one launch (start us, length us, event | category | flops | bytes accessed | tf_op | source)
XLA Modules:
  0.0 176.8 jit_solution(3467493316059481468)
XLA Ops:
  3.5 2.1 %fusion.90 = (f32[16,16,384]{2,1,0:T(8,128)}, f32[16,16,384]{2,1,0:T(8,128)}) fusion(f32[16,16]{1,0:T(8,128)S(1)} %get-tuple-element.865, f32[384]{0:T(512)S(1)} %get-tuple-element.858, f32[16,16]{1,0:T(8,128)S(1)} %get-tuple-element.859), kind=kLoop, calls=%fused_computation.125 | loop fusion | flops 7274496 | bytes 790016 | tf_op jit(solution)/shard_map/mul | solution.py:28
  10.6 165.1 %while.21 = (s32[]{:T(128)}, f32[2,16,16,384]{3,2,1,0:T(8,128)}, f32[2,16,16,384]{3,2,1,0:T(8,128)S(1)}, f32[16,16,384]{2,1,0:T(8,128)}, f32[16,16,384]{2,1,0:T(...) while((s32[]{:T(128)}, f32[2,16,16,384]{3,2,1,0:T(8,128)}, ...), condition=%wide.region_3.5_spmd.clone.clone.clone, body=%wide.region_2.4_spmd.clone.clone.clone.sunk | while | flops 3361161216 | bytes 56363244 | solution.py:148
  11.1 2.6 %convolution_bitcast_fusion.13 = f32[6,2,8,384]{3,2,1,0:T(8,128)S(1)} fusion(f32[384]{0:T(512)S(1)} %get-tuple-element.916, f32[384]{0:T(512)S(1)} %get-tuple-element.917, f32[384]{0:T(512)S(1)} %get-tuple-element.918, f32[16,6,384]{2,1,0:T(8,128)S(1)} %convolution_bitcast_fusion.12), kind=kOutput, calls=%fused_computation.26.clone.1 | convolution fusion | flops 170311680 | bytes 299520 | tf_op jit(solution)/shard_map/while/body/eval_jaxpr/iyk,kz->iyz/dot_general | solution.py:47
  13.7 3.1 %collective-permute-start.1 = (f32[16,2304]{1,0:T(8,128)S(1)}, f32[16,2304]{1,0:T(8,128)}, u32[]{:S(2)}, u32[]{:S(2)}) collective-permute-start(f32[16,2304]{1,0:T(8,128)S(1)} %bitcast.227), channel_id=1, source_target_pairs={{0,3},{1,0},{2,1},{3,2},{4,7},{5,4},{6,5},{7,6},{8,11},{9,8},{10,9... | collective-permute-start | bytes 442376 | tf_op jit(solution)/shard_map/while/body/eval_jaxpr/ppermute | solution.py:55
  16.8 2.2 %collective-permute-start.2 = (f32[16,2304]{1,0:T(8,128)S(1)}, f32[16,2304]{1,0:T(8,128)}, u32[]{:S(2)}, u32[]{:S(2)}) collective-permute-start(f32[16,2304]{1,0:T(8,128)S(1)} %bitcast.229), channel_id=1, source_target_pairs={{0,2},{1,3},{2,0},{3,1},{4,6},{5,7},{6,4},{7,5},{8,10},{9,11},{10,... | collective-permute-start | bytes 442376 | tf_op jit(solution)/shard_map/while/body/eval_jaxpr/ppermute | solution.py:55
  20.1 3.3 %fusion.217 = f32[8,3,8,2,384]{4,2,3,1,0:T(8,128)S(1)} fusion(f32[8,3,8,2,384]{4,3,2,1,0:T(2,128)S(1)} %dot_general.139, f32[384]{0:T(512)S(1)} %get-tuple-element.916, f32[384]{0:T(512)S(1)} %get-tuple-element.917, f32[384]{0:T(512)S(1)} %get-tuple-element.918), kind=kOutput, calls=%fused_computation.37.clone.1 | convolution fusion | flops 679919616 | bytes 1184256 | tf_op jit(solution)/shard_map/while/body/eval_jaxpr/rz,zk->rk/dot_general | solution.py:47
  24.9 1.7 collective-permute-done
  29.4 2.7 %convolution_bitcast_fusion.15 = f32[128,3,2,384]{0,3,1,2:T(8,128)S(1)} fusion(s32[12,8]{1,0:T(8,128)} %get-tuple-element.919, f32[4,3,8,2,384]{4,2,3,1,0:T(8,128)S(1)} %copy.87, f32[8,3,8,2,384]{4,2,3,1,0:T(8,128)S(1)} %fusion.217), kind=kOutput, calls=%fused_computation.14.clone.1 | convolution fusion | flops 339984384 | bytes 2064768 | tf_op jit(solution)/shard_map/while/body/eval_jaxpr/sfq,fmqcz->smcz/dot_general | solution.py:47
  32.1 2.0 %copy.88 = f32[128,3,2,384]{3,2,1,0:T(2,128)} copy(f32[128,3,2,384]{0,3,1,2:T(8,128)S(1)} %convolution_bitcast_fusion.15) | data formatting | bytes 2359296 | tf_op jit(solution)/shard_map/while/body/eval_jaxpr/sfq,fmqcz->smcz/dot_general | solution.py:47
  34.1 12.0 %all-to-all-start = ((f32[128,3,2,384]{3,2,1,0:T(2,128)}), f32[128,3,2,384]{3,2,1,0:T(2,128)S(1)}, u32[]{:S(2)}, u32[]{:S(2)}) async-start(f32[128,3,2,384]{3,2,1,0:T(2,128)} %copy.88), calls=%async_computation | async-start | bytes 2359296 | tf_op jit(solution)/shard_map/while/body/eval_jaxpr/all_to_all | solution.py:131
  46.9 2.2 %cosine_multiply_fusion.10 = f32[16,16,384]{2,1,0:T(8,128)} fusion(f32[384]{0:T(512)S(1)} %get-tuple-element.914, f32[16,16]{1,0:T(8,128)S(1)} %get-tuple-element.915), kind=kLoop, calls=%fused_computation.46.clone.1 | loop fusion | flops 294912 | bytes 395776 | tf_op jit(solution)/shard_map/mul | solution.py:27
  49.2 28.6 %all-to-all-done = f32[128,3,2,384]{3,2,1,0:T(2,128)S(1)} async-done(((f32[128,3,2,384]{3,2,1,0:T(2,128)}), f32[128,3,2,384]{3,2,1,0:T(2,128)S(1)}, u32[]{:S(2)}, u32[]{:S(2)}) %all-to-all-start) | async-done | bytes 1179680 | tf_op jit(solution)/shard_map/while/body/eval_jaxpr/all_to_all | solution.py:131
  80.0 2.8 %convolution_bitcast_fusion.16 = f32[16,2,3,384]{3,0,2,1:T(8,128)S(1)} fusion(f32[12,1,16,384]{3,2,1,0:T(8,128)S(1)} %get-tuple-element.837, f32[12,1,16,384]{3,2,1,0:T(8,128)S(1)} %get-tuple-element.838, f32[12,1,16,384]{3,2,1,0:T(8,128)S(1)} %get-tuple-element.839, f32[384]{0:T(512)S(1)} %get-tuple-element.916, f32[384]{0:T(512)S(1)} %get-tuple-element.917, ...), kind=kOutput, calls=%fused_computation.25.clone.1 | convolution fusion | flops 170754048 | bytes 1036800 | tf_op jit(solution)/shard_map/while/body/eval_jaxpr/fmxz,kz->xfmk/dot_general | solution.py:47
  83.6 1.5 collective-permute-start.4
  86.6 3.3 %fusion.220 = f32[2,192,384]{2,1,0:T(8,128)S(1)} fusion(f32[2,192,384]{2,1,0:T(8,128)S(1)} %bitcast.225, f32[384]{0:T(512)S(1)} %get-tuple-element.916, f32[384]{0:T(512)S(1)} %get-tuple-element.917, f32[384]{0:T(512)S(1)} %get-tuple-element.918), kind=kOutput, calls=%fused_computation.39.clone.1 | convolution fusion | flops 679919616 | bytes 1184256 | tf_op jit(solution)/shard_map/while/body/eval_jaxpr/rz,kz->rk/dot_general | solution.py:47
  92.0 1.2 fusion.223
  94.5 1.9 %fusion.225 = f32[16,16,384]{2,1,0:T(8,128)S(1)} fusion(f32[16,16,384]{2,1,0:T(8,128)S(1)} %copy-done.6, f32[16,6,384]{2,1,0:T(8,128)S(1)} %reshape.560, f32[16,16,384]{2,1,0:T(8,128)S(1)} %copy-done.7, f32[16,16,384]{2,1,0:T(8,128)S(1)} %get-tuple-element.872, f32[16,16]{1,0:T(8,128)S(1)} %get-tuple-element.921, f32[384]{0:T(512)S(1)} %get-tuple-element.914, ...), kind=kOutput, calls=%fused_computation.21.clone.1 | convolution fusion | flops 7766016 | bytes 1723264 | tf_op jit(solution)/shard_map/while/body/eval_jaxpr/iyk,jy->ijk/dot_general | solution.py:47
  97.5 2.6 %convolution_bitcast_fusion.13 = f32[6,2,8,384]{3,2,1,0:T(8,128)S(1)} fusion(f32[384]{0:T(512)S(1)} %get-tuple-element.916, f32[384]{0:T(512)S(1)} %get-tuple-element.917, f32[384]{0:T(512)S(1)} %get-tuple-element.918, f32[16,6,384]{2,1,0:T(8,128)S(1)} %convolution_bitcast_fusion.12), kind=kOutput, calls=%fused_computation.26.clone.1 | convolution fusion | flops 170311680 | bytes 299520 | tf_op jit(solution)/shard_map/while/body/eval_jaxpr/iyk,kz->iyz/dot_general | solution.py:47
  100.1 1.8 %collective-permute-start.1 = (f32[16,2304]{1,0:T(8,128)S(1)}, f32[16,2304]{1,0:T(8,128)}, u32[]{:S(2)}, u32[]{:S(2)}) collective-permute-start(f32[16,2304]{1,0:T(8,128)S(1)} %bitcast.227), channel_id=1, source_target_pairs={{0,3},{1,0},{2,1},{3,2},{4,7},{5,4},{6,5},{7,6},{8,11},{9,8},{10,9... | collective-permute-start | bytes 442376 | tf_op jit(solution)/shard_map/while/body/eval_jaxpr/ppermute | solution.py:55
  102.6 2.0 %collective-permute-start.2 = (f32[16,2304]{1,0:T(8,128)S(1)}, f32[16,2304]{1,0:T(8,128)}, u32[]{:S(2)}, u32[]{:S(2)}) collective-permute-start(f32[16,2304]{1,0:T(8,128)S(1)} %bitcast.229), channel_id=1, source_target_pairs={{0,2},{1,3},{2,0},{3,1},{4,6},{5,7},{6,4},{7,5},{8,10},{9,11},{10,... | collective-permute-start | bytes 442376 | tf_op jit(solution)/shard_map/while/body/eval_jaxpr/ppermute | solution.py:55
  105.7 3.3 %fusion.217 = f32[8,3,8,2,384]{4,2,3,1,0:T(8,128)S(1)} fusion(f32[8,3,8,2,384]{4,3,2,1,0:T(2,128)S(1)} %dot_general.139, f32[384]{0:T(512)S(1)} %get-tuple-element.916, f32[384]{0:T(512)S(1)} %get-tuple-element.917, f32[384]{0:T(512)S(1)} %get-tuple-element.918), kind=kOutput, calls=%fused_computation.37.clone.1 | convolution fusion | flops 679919616 | bytes 1184256 | tf_op jit(solution)/shard_map/while/body/eval_jaxpr/rz,zk->rk/dot_general | solution.py:47
  113.2 2.7 %convolution_bitcast_fusion.15 = f32[128,3,2,384]{0,3,1,2:T(8,128)S(1)} fusion(s32[12,8]{1,0:T(8,128)} %get-tuple-element.919, f32[4,3,8,2,384]{4,2,3,1,0:T(8,128)S(1)} %copy.87, f32[8,3,8,2,384]{4,2,3,1,0:T(8,128)S(1)} %fusion.217), kind=kOutput, calls=%fused_computation.14.clone.1 | convolution fusion | flops 339984384 | bytes 2064768 | tf_op jit(solution)/shard_map/while/body/eval_jaxpr/sfq,fmqcz->smcz/dot_general | solution.py:47
  116.0 2.0 %copy.88 = f32[128,3,2,384]{3,2,1,0:T(2,128)} copy(f32[128,3,2,384]{0,3,1,2:T(8,128)S(1)} %convolution_bitcast_fusion.15) | data formatting | bytes 2359296 | tf_op jit(solution)/shard_map/while/body/eval_jaxpr/sfq,fmqcz->smcz/dot_general | solution.py:47
  118.0 5.9 %all-to-all-start = ((f32[128,3,2,384]{3,2,1,0:T(2,128)}), f32[128,3,2,384]{3,2,1,0:T(2,128)S(1)}, u32[]{:S(2)}, u32[]{:S(2)}) async-start(f32[128,3,2,384]{3,2,1,0:T(2,128)} %copy.88), calls=%async_computation | async-start | bytes 2359296 | tf_op jit(solution)/shard_map/while/body/eval_jaxpr/all_to_all | solution.py:131
  124.7 2.2 %cosine_multiply_fusion.10 = f32[16,16,384]{2,1,0:T(8,128)} fusion(f32[384]{0:T(512)S(1)} %get-tuple-element.914, f32[16,16]{1,0:T(8,128)S(1)} %get-tuple-element.915), kind=kLoop, calls=%fused_computation.46.clone.1 | loop fusion | flops 294912 | bytes 395776 | tf_op jit(solution)/shard_map/mul | solution.py:27
  126.9 28.6 %all-to-all-done = f32[128,3,2,384]{3,2,1,0:T(2,128)S(1)} async-done(((f32[128,3,2,384]{3,2,1,0:T(2,128)}), f32[128,3,2,384]{3,2,1,0:T(2,128)S(1)}, u32[]{:S(2)}, u32[]{:S(2)}) %all-to-all-start) | async-done | bytes 1179680 | tf_op jit(solution)/shard_map/while/body/eval_jaxpr/all_to_all | solution.py:131
  157.7 2.8 %convolution_bitcast_fusion.16 = f32[16,2,3,384]{3,0,2,1:T(8,128)S(1)} fusion(f32[12,1,16,384]{3,2,1,0:T(8,128)S(1)} %get-tuple-element.837, f32[12,1,16,384]{3,2,1,0:T(8,128)S(1)} %get-tuple-element.838, f32[12,1,16,384]{3,2,1,0:T(8,128)S(1)} %get-tuple-element.839, f32[384]{0:T(512)S(1)} %get-tuple-element.916, f32[384]{0:T(512)S(1)} %get-tuple-element.917, ...), kind=kOutput, calls=%fused_computation.25.clone.1 | convolution fusion | flops 170754048 | bytes 1036800 | tf_op jit(solution)/shard_map/while/body/eval_jaxpr/fmxz,kz->xfmk/dot_general | solution.py:47
  161.3 2.4 %collective-permute-start.4 = (f32[16,2304]{1,0:T(8,128)}, f32[16,2304]{1,0:T(8,128)S(1)}, u32[]{:S(2)}, u32[]{:S(2)}) collective-permute-start(f32[16,2304]{1,0:T(8,128)} %reshape.559), channel_id=1, source_target_pairs={{0,3},{1,0},{2,1},{3,2},{4,7},{5,4},{6,5},{7,6},{8,11},{9,8},{10,9... | collective-permute-start | bytes 442376 | tf_op jit(solution)/shard_map/while/body/eval_jaxpr/ppermute | solution.py:55
  163.7 1.5 collective-permute-start.5
  165.2 3.3 %fusion.220 = f32[2,192,384]{2,1,0:T(8,128)S(1)} fusion(f32[2,192,384]{2,1,0:T(8,128)S(1)} %bitcast.225, f32[384]{0:T(512)S(1)} %get-tuple-element.916, f32[384]{0:T(512)S(1)} %get-tuple-element.917, f32[384]{0:T(512)S(1)} %get-tuple-element.918), kind=kOutput, calls=%fused_computation.39.clone.1 | convolution fusion | flops 679919616 | bytes 1184256 | tf_op jit(solution)/shard_map/while/body/eval_jaxpr/rz,kz->rk/dot_general | solution.py:47
  170.6 1.2 fusion.223
  173.1 1.9 %fusion.225 = f32[16,16,384]{2,1,0:T(8,128)S(1)} fusion(f32[16,16,384]{2,1,0:T(8,128)S(1)} %copy-done.6, f32[16,6,384]{2,1,0:T(8,128)S(1)} %reshape.560, f32[16,16,384]{2,1,0:T(8,128)S(1)} %copy-done.7, f32[16,16,384]{2,1,0:T(8,128)S(1)} %get-tuple-element.872, f32[16,16]{1,0:T(8,128)S(1)} %get-tuple-element.921, f32[384]{0:T(512)S(1)} %get-tuple-element.914, ...), kind=kOutput, calls=%fused_computation.21.clone.1 | convolution fusion | flops 7766016 | bytes 1723264 | tf_op jit(solution)/shard_map/while/body/eval_jaxpr/iyk,jy->ijk/dot_general | solution.py:47
  (158 shorter events, 37.6 us)
Async XLA Ops:
  0.6 1.1 copy-start.9
  0.6 2.0 %copy-start.10 = (f32[1,16,16,384]{3,2,1,0:T(8,128)S(1)}, f32[1,16,16,384]{3,2,1,0:T(8,128)}, u32[]{:S(2)}) copy-start(f32[1,16,16,384]{3,2,1,0:T(8,128)} %param.12) | copy-start | bytes 1179652
  2.6 3.1 %copy-start.13 = (s32[6]{0:T(128)S(1)}, s32[6]{0:T(128)}, u32[]{:S(2)}) copy-start(s32[6]{0:T(128)} %constant.191) | copy-start | bytes 76
  6.5 1.5 copy-start.14
  6.5 4.1 %copy-start.1 = (f32[2,16,16,384]{3,2,1,0:T(8,128)S(1)}, f32[2,16,16,384]{3,2,1,0:T(8,128)}, u32[]{:S(2)}) copy-start(f32[2,16,16,384]{3,2,1,0:T(8,128)} %param.9) | copy-start | bytes 2359300
  6.5 4.1 %copy-start.3 = (f32[1,16,16,384]{3,2,1,0:T(8,128)S(1)}, f32[1,16,16,384]{3,2,1,0:T(8,128)}, u32[]{:S(2)}) copy-start(f32[1,16,16,384]{3,2,1,0:T(8,128)} %param.11) | copy-start | bytes 1179652
  10.8 9.0 %copy-start.11 = (pred[12,1,8,1,1]{0,2,4,3,1:T(8,128)(4,1)}, pred[12,1,8,1,1]{0,2,4,3,1:T(8,128)(4,1)S(1)}, u32[]{:S(2)}) copy-start(pred[12,1,8,1,1]{0,2,4,3,1:T(8,128)(4,1)S(1)} %get-tuple-element.902) | copy-start | bytes 292 | tf_op jit(solution)/shard_map/while
  13.7 10.0 %collective-permute-start.1 = (f32[16,2304]{1,0:T(8,128)S(1)}, f32[16,2304]{1,0:T(8,128)}, u32[]{:S(2)}, u32[]{:S(2)}) collective-permute-start(f32[16,2304]{1,0:T(8,128)S(1)} %bitcast.227), channel_id=1, source_target_pairs={{0,3},{1,0},{2,1},{3,2},{4,7},{5,4},{6,5},{7,6},{8,11},{9,8},{10,9... | collective-permute-start | bytes 442376 | tf_op jit(solution)/shard_map/while/body/eval_jaxpr/ppermute | solution.py:55
  16.8 9.8 %collective-permute-start = (f32[16,2304]{1,0:T(8,128)S(1)}, f32[16,2304]{1,0:T(8,128)}, u32[]{:S(2)}, u32[]{:S(2)}) collective-permute-start(f32[16,2304]{1,0:T(8,128)S(1)} %bitcast.228), channel_id=1, source_target_pairs={{0,1},{1,2},{2,3},{3,0},{4,5},{5,6},{6,7},{7,4},{8,9},{9,10},{10,1... | collective-permute-start | bytes 442376 | tf_op jit(solution)/shard_map/while/body/eval_jaxpr/ppermute | solution.py:55
  16.8 11.0 %collective-permute-start.2 = (f32[16,2304]{1,0:T(8,128)S(1)}, f32[16,2304]{1,0:T(8,128)}, u32[]{:S(2)}, u32[]{:S(2)}) collective-permute-start(f32[16,2304]{1,0:T(8,128)S(1)} %bitcast.229), channel_id=1, source_target_pairs={{0,2},{1,3},{2,0},{3,1},{4,6},{5,7},{6,4},{7,5},{8,10},{9,11},{10,... | collective-permute-start | bytes 442376 | tf_op jit(solution)/shard_map/while/body/eval_jaxpr/ppermute | solution.py:55
  34.1 43.6 %all-to-all-start = ((f32[128,3,2,384]{3,2,1,0:T(2,128)}), f32[128,3,2,384]{3,2,1,0:T(2,128)S(1)}, u32[]{:S(2)}, u32[]{:S(2)}) async-start(f32[128,3,2,384]{3,2,1,0:T(2,128)} %copy.88), calls=%async_computation | async-start | bytes 2359296 | tf_op jit(solution)/shard_map/while/body/eval_jaxpr/all_to_all | solution.py:131
  83.6 9.7 %collective-permute-start.4 = (f32[16,2304]{1,0:T(8,128)}, f32[16,2304]{1,0:T(8,128)S(1)}, u32[]{:S(2)}, u32[]{:S(2)}) collective-permute-start(f32[16,2304]{1,0:T(8,128)} %reshape.559), channel_id=1, source_target_pairs={{0,3},{1,0},{2,1},{3,2},{4,7},{5,4},{6,5},{7,6},{8,11},{9,8},{10,9... | collective-permute-start | bytes 442376 | tf_op jit(solution)/shard_map/while/body/eval_jaxpr/ppermute | solution.py:55
  85.1 8.8 %collective-permute-start.3 = (f32[16,2304]{1,0:T(8,128)}, f32[16,2304]{1,0:T(8,128)S(1)}, u32[]{:S(2)}, u32[]{:S(2)}) collective-permute-start(f32[16,2304]{1,0:T(8,128)} %reshape.559), channel_id=1, source_target_pairs={{0,1},{1,2},{2,3},{3,0},{4,5},{5,6},{6,7},{7,4},{8,9},{9,10},{10,1... | collective-permute-start | bytes 442376 | tf_op jit(solution)/shard_map/while/body/eval_jaxpr/ppermute | solution.py:55
  85.6 8.5 %collective-permute-start.5 = (f32[16,2304]{1,0:T(8,128)}, f32[16,2304]{1,0:T(8,128)S(1)}, u32[]{:S(2)}, u32[]{:S(2)}) collective-permute-start(f32[16,2304]{1,0:T(8,128)} %reshape.559), channel_id=1, source_target_pairs={{0,2},{1,3},{2,0},{3,1},{4,6},{5,7},{6,4},{7,5},{8,10},{9,11},{10,... | collective-permute-start | bytes 442376 | tf_op jit(solution)/shard_map/while/body/eval_jaxpr/ppermute | solution.py:55
  86.6 4.2 %copy-start.4 = (f32[16,16,384]{2,1,0:T(8,128)S(1)}, f32[16,16,384]{2,1,0:T(8,128)}, u32[]{:S(2)}) copy-start(f32[16,16,384]{2,1,0:T(8,128)} %cosine_multiply_fusion.10) | copy-start | bytes 1179652 | tf_op jit(solution)/shard_map/while
  86.6 4.2 %copy-start.5 = (f32[2,16,16,384]{3,2,1,0:T(8,128)S(1)}, f32[2,16,16,384]{3,2,1,0:T(8,128)}, u32[]{:S(2)}) copy-start(f32[2,16,16,384]{3,2,1,0:T(8,128)} %get-tuple-element.869) | copy-start | bytes 2359300 | tf_op jit(solution)/shard_map/while
  86.6 4.2 %copy-start.8 = (f32[16,16,384]{2,1,0:T(8,128)S(1)}, f32[16,16,384]{2,1,0:T(8,128)}, u32[]{:S(2)}) copy-start(f32[16,16,384]{2,1,0:T(8,128)} %get-tuple-element.901) | copy-start | bytes 1179652 | tf_op jit(solution)/shard_map/while
  92.0 2.5 %copy-start.6 = (f32[16,16,384]{2,1,0:T(8,128)S(1)}, f32[16,16,384]{2,1,0:T(8,128)}, u32[]{:S(2)}) copy-start(f32[16,16,384]{2,1,0:T(8,128)} %get-tuple-element.913) | copy-start | bytes 1179652 | tf_op jit(solution)/shard_map/while
  92.0 2.5 %copy-start.7 = (f32[16,16,384]{2,1,0:T(8,128)S(1)}, f32[16,16,384]{2,1,0:T(8,128)}, u32[]{:S(2)}) copy-start(f32[16,16,384]{2,1,0:T(8,128)} %get-tuple-element.871) | copy-start | bytes 1179652 | tf_op jit(solution)/shard_map/while
  97.1 8.2 %copy-start.11 = (pred[12,1,8,1,1]{0,2,4,3,1:T(8,128)(4,1)}, pred[12,1,8,1,1]{0,2,4,3,1:T(8,128)(4,1)S(1)}, u32[]{:S(2)}) copy-start(pred[12,1,8,1,1]{0,2,4,3,1:T(8,128)(4,1)S(1)} %get-tuple-element.902) | copy-start | bytes 292 | tf_op jit(solution)/shard_map/while
  100.1 9.2 %collective-permute-start.1 = (f32[16,2304]{1,0:T(8,128)S(1)}, f32[16,2304]{1,0:T(8,128)}, u32[]{:S(2)}, u32[]{:S(2)}) collective-permute-start(f32[16,2304]{1,0:T(8,128)S(1)} %bitcast.227), channel_id=1, source_target_pairs={{0,3},{1,0},{2,1},{3,2},{4,7},{5,4},{6,5},{7,6},{8,11},{9,8},{10,9... | collective-permute-start | bytes 442376 | tf_op jit(solution)/shard_map/while/body/eval_jaxpr/ppermute | solution.py:55
  101.9 8.6 %collective-permute-start = (f32[16,2304]{1,0:T(8,128)S(1)}, f32[16,2304]{1,0:T(8,128)}, u32[]{:S(2)}, u32[]{:S(2)}) collective-permute-start(f32[16,2304]{1,0:T(8,128)S(1)} %bitcast.228), channel_id=1, source_target_pairs={{0,1},{1,2},{2,3},{3,0},{4,5},{5,6},{6,7},{7,4},{8,9},{9,10},{10,1... | collective-permute-start | bytes 442376 | tf_op jit(solution)/shard_map/while/body/eval_jaxpr/ppermute | solution.py:55
  102.6 9.1 %collective-permute-start.2 = (f32[16,2304]{1,0:T(8,128)S(1)}, f32[16,2304]{1,0:T(8,128)}, u32[]{:S(2)}, u32[]{:S(2)}) collective-permute-start(f32[16,2304]{1,0:T(8,128)S(1)} %bitcast.229), channel_id=1, source_target_pairs={{0,2},{1,3},{2,0},{3,1},{4,6},{5,7},{6,4},{7,5},{8,10},{9,11},{10,... | collective-permute-start | bytes 442376 | tf_op jit(solution)/shard_map/while/body/eval_jaxpr/ppermute | solution.py:55
  118.0 37.5 %all-to-all-start = ((f32[128,3,2,384]{3,2,1,0:T(2,128)}), f32[128,3,2,384]{3,2,1,0:T(2,128)S(1)}, u32[]{:S(2)}, u32[]{:S(2)}) async-start(f32[128,3,2,384]{3,2,1,0:T(2,128)} %copy.88), calls=%async_computation | async-start | bytes 2359296 | tf_op jit(solution)/shard_map/while/body/eval_jaxpr/all_to_all | solution.py:131
  161.3 10.6 %collective-permute-start.4 = (f32[16,2304]{1,0:T(8,128)}, f32[16,2304]{1,0:T(8,128)S(1)}, u32[]{:S(2)}, u32[]{:S(2)}) collective-permute-start(f32[16,2304]{1,0:T(8,128)} %reshape.559), channel_id=1, source_target_pairs={{0,3},{1,0},{2,1},{3,2},{4,7},{5,4},{6,5},{7,6},{8,11},{9,8},{10,9... | collective-permute-start | bytes 442376 | tf_op jit(solution)/shard_map/while/body/eval_jaxpr/ppermute | solution.py:55
  163.7 8.8 %collective-permute-start.3 = (f32[16,2304]{1,0:T(8,128)}, f32[16,2304]{1,0:T(8,128)S(1)}, u32[]{:S(2)}, u32[]{:S(2)}) collective-permute-start(f32[16,2304]{1,0:T(8,128)} %reshape.559), channel_id=1, source_target_pairs={{0,1},{1,2},{2,3},{3,0},{4,5},{5,6},{6,7},{7,4},{8,9},{9,10},{10,1... | collective-permute-start | bytes 442376 | tf_op jit(solution)/shard_map/while/body/eval_jaxpr/ppermute | solution.py:55
  163.7 9.1 %collective-permute-start.5 = (f32[16,2304]{1,0:T(8,128)}, f32[16,2304]{1,0:T(8,128)S(1)}, u32[]{:S(2)}, u32[]{:S(2)}) collective-permute-start(f32[16,2304]{1,0:T(8,128)} %reshape.559), channel_id=1, source_target_pairs={{0,2},{1,3},{2,0},{3,1},{4,6},{5,7},{6,4},{7,5},{8,10},{9,11},{10,... | collective-permute-start | bytes 442376 | tf_op jit(solution)/shard_map/while/body/eval_jaxpr/ppermute | solution.py:55
  165.2 4.2 %copy-start.4 = (f32[16,16,384]{2,1,0:T(8,128)S(1)}, f32[16,16,384]{2,1,0:T(8,128)}, u32[]{:S(2)}) copy-start(f32[16,16,384]{2,1,0:T(8,128)} %cosine_multiply_fusion.10) | copy-start | bytes 1179652 | tf_op jit(solution)/shard_map/while
  165.2 4.2 %copy-start.5 = (f32[2,16,16,384]{3,2,1,0:T(8,128)S(1)}, f32[2,16,16,384]{3,2,1,0:T(8,128)}, u32[]{:S(2)}) copy-start(f32[2,16,16,384]{3,2,1,0:T(8,128)} %get-tuple-element.869) | copy-start | bytes 2359300 | tf_op jit(solution)/shard_map/while
  165.2 4.2 %copy-start.8 = (f32[16,16,384]{2,1,0:T(8,128)S(1)}, f32[16,16,384]{2,1,0:T(8,128)}, u32[]{:S(2)}) copy-start(f32[16,16,384]{2,1,0:T(8,128)} %get-tuple-element.901) | copy-start | bytes 1179652 | tf_op jit(solution)/shard_map/while
  170.6 2.5 %copy-start.6 = (f32[16,16,384]{2,1,0:T(8,128)S(1)}, f32[16,16,384]{2,1,0:T(8,128)}, u32[]{:S(2)}) copy-start(f32[16,16,384]{2,1,0:T(8,128)} %get-tuple-element.913) | copy-start | bytes 1179652 | tf_op jit(solution)/shard_map/while
  170.6 2.5 %copy-start.7 = (f32[16,16,384]{2,1,0:T(8,128)S(1)}, f32[16,16,384]{2,1,0:T(8,128)}, u32[]{:S(2)}) copy-start(f32[16,16,384]{2,1,0:T(8,128)} %get-tuple-element.871) | copy-start | bytes 1179652 | tf_op jit(solution)/shard_map/while
  (4 other events, 3.5 us)

commit v2 on v0

--- a/solution.py
+++ b/solution.py
@@ -110,7 +110,9 @@
     )
 
     def time_step(_, state):
-        small_old, small_cur, plaza_old, plaza_cur = state
+        small_cur, small_step, plaza_cur, plaza_step = state
+        small_old = small_cur - small_step
+        plaza_old = plaza_cur - plaza_step
         flat_modes = small_cur.reshape(owned, edge * edge, height)
         small_strips = ein("rz,zk->rk", ein("pr,bpk->brk", face_rows, flat_modes).reshape(-1, height), table_height)
         small_strips = small_strips.reshape(owned * 4, 3, edge, height)
@@ -138,11 +140,12 @@
         plaza_force = ein("iyk,jy->ijk", plaza_x, side6)
         small_next = small_cos * small_cur - small_old + small_gain * small_force
         plaza_next = plaza_cos * plaza_cur - plaza_old + plaza_gain * plaza_force
-        return (small_cur, small_next, plaza_cur, plaza_next)
+        return (small_next, small_next - small_cur, plaza_next, plaza_next - plaza_cur)
 
-    small_old, small_cur, plaza_old, plaza_cur = lax.fori_loop(
-        0, STEPS, time_step, (small_prev, small_now, plaza_prev[0], plaza_now[0])
-    )
+    start = (small_now, small_now - small_prev, plaza_now[0], plaza_now[0] - plaza_prev[0])
+    small_cur, small_step, plaza_cur, plaza_step = lax.fori_loop(0, STEPS, time_step, start)
+    small_old = small_cur - small_step
+    plaza_old = plaza_cur - plaza_step
     return (small_cur, small_old, plaza_cur[None], plaza_old[None])
 
 

time: 172 us -> 195 us (1.13)
  matrix products: 39.6 us -> 52.6 us
  other arithmetic: 8.66 us -> 19.3 us
  waiting for transfers between devices: 59.6 us -> 56.3 us
  local copies, waits for them, and re-layouts: 25 us -> 27.3 us
    dot_general x24, matrix products: 39.6 us -> 52.6 us  [ein(): jnp.einsum(spec, a, b, precision=highest, preferred_element_type=jnp.floa...]
    sub x0 -> x5, other arithmetic: none -> 5.32 us  [the longest x1 2.16 us: on_device(): small_now - small_prev]
    dot_general x4, local copies, waits for them, and re-layouts: 4.65 us -> 7.55 us  [ein(): jnp.einsum(spec, a, b, precision=highest, preferred_element_type=jnp.floa...]
    while x36 -> x60, local copies, waits for them, and re-layouts: 4.23 us -> 1.44 us
    broadcast_in_dim x2, local copies, waits for them, and re-layouts: 0.2 us -> 2.63 us  [time_step(): difference = jnp.where(pair_mask, remote - segments, 0.0)]
    all_to_all x2, waiting for transfers between devices: 58.6 us -> 56.3 us  [time_step(): arrived = lax.all_to_all(outgoing, 'rect', 0, 0, tiled=True)]
    broadcast_in_dim x0 -> x1, other arithmetic: none -> 2.16 us  [on_device(): return (small_cur, small_old, plaza_cur[None], plaza_old[None])]
    unnamed x20 -> x22, local copies, waits for them, and re-layouts: 4.39 us -> 2.46 us
  transfers between devices with their start and end apart: 14 -> 14, of which waited for: 5 -> 3; matrix products, arithmetic and copies ran while one was open for 16% -> 17% of each run, Pallas kernels for 0% -> 0%
where the time goes in v2:
time: 195 us; the launch traced here: 194 us
  waiting for transfers between devices  56.3 us (29%)
  matrix products  52.6 us (27%)
  starting transfers between devices  36.4 us (19%)
  local copies, waits for them, and re-layouts  27.3 us (14%)
  other arithmetic  19.3 us (10%)
    all_to_all x2, waiting for transfers between devices, time_step(): arrived = lax.all_to_all(outgoing, 'rect', 0, 0, tiled=True)  56.3 us
    dot_general x24, matrix products, ein(): jnp.einsum(spec, a, b, precision=highest, preferred_element_type=jnp.floa...  52.6 us
    ppermute x12, starting transfers between devices, gather_slabs(): pieces.append(lax.ppermute(block, 'split', perm))  18.7 us
    all_to_all x2, starting transfers between devices, time_step(): arrived = lax.all_to_all(outgoing, 'rect', 0, 0, tiled=True)  17.7 us
    dot_general x4, local copies, waits for them, and re-layouts, ein(): jnp.einsum(spec, a, b, precision=highest, preferred_element_type=jnp.floa...  7.55 us
    concatenate x12, local copies, waits for them, and re-layouts, gather_slabs(): return jnp.concatenate(pieces, axis=0)  5.59 us
    mul x2, other arithmetic, update_factors(): twice_cos = 2.0 * jnp.cos(phase_angle)  4.31 us
  transfers between devices with their start and end apart: 14, of which 3 were waited for; matrix products, arithmetic and copies ran while one was open for 17% of the time, Pallas kernels for 0%

profile of v2, /device:TPU:2, one launch (start us, length us, event | category | flops | bytes accessed | tf_op | source)
XLA Modules:
  0.0 193.6 jit_solution(9244127275367578291)
XLA Ops:
  3.2 2.8 %fusion.129 = (f32[16,16,384]{2,1,0:T(8,128)}, f32[16,16,384]{2,1,0:T(8,128)}) fusion(f32[16,16]{1,0:T(8,128)} %get-tuple-element.758, f32[384]{0:T(512)S(1)} %get-tuple-element.748, f32[16,16]{1,0:T(8,128)} %get-tuple-element.749), kind=kLoop, calls=%fused_computation.165 | loop fusion | flops 7274496 | bytes 790016 | tf_op jit(solution)/shard_map/mul | solution.py:28
  12.5 2.2 %sub.75 = f32[2,16,16,384]{3,2,1,0:T(8,128)} subtract(f32[2,16,16,384]{3,2,1,0:T(8,128)S(1)} %copy.159, f32[2,16,16,384]{3,2,1,0:T(8,128)} %param.10) | non-fusion elementwise | flops 196608 | bytes 2359296 | tf_op jit(solution)/shard_map/sub | solution.py:145
  16.8 173.6 %while.21 = (s32[]{:T(128)}, f32[2,16,16,384]{3,2,1,0:T(8,128)S(1)}, f32[2,16,16,384]{3,2,1,0:T(8,128)}, f32[16,16,384]{2,1,0:T(8,128)S(1)}, f32[16,16,384]{2,1,...) while((s32[]{:T(128)}, ...), condition=%wide.region_3.5_spmd.clone.clone.clone, body=%wide.region_2.4_spmd.clone.clone.clone.sunk | while | flops 3362420736 | bytes 54597500 | solution.py:146
  17.1 3.3 %fusion.202 = f32[16,6,384]{2,0,1:T(8,128)S(1)} fusion(f32[384]{0:T(512)} %get-tuple-element.802, f32[384]{0:T(512)} %get-tuple-element.803, f32[384]{0:T(512)S(1)} %get-tuple-element.804, f32[16,6,384]{2,1,0:T(8,128)S(1)} %convolution_bitcast_fusion.12), kind=kOutput, calls=%fused_computation.50.clone.1 | convolution fusion | flops 170311680 | bytes 299520 | tf_op jit(solution)/shard_map/while/body/eval_jaxpr/iyk,kz->iyz/dot_general | solution.py:47
  20.4 1.7 collective-permute-start
  22.1 2.9 %collective-permute-start.1 = (f32[16,2304]{1,0:T(8,128)S(1)}, f32[16,2304]{1,0:T(8,128)}, u32[]{:S(2)}, u32[]{:S(2)}) collective-permute-start(f32[16,2304]{1,0:T(8,128)S(1)} %bitcast.231), channel_id=1, source_target_pairs={{0,2},{1,3},{2,0},{3,1},{4,6},{5,7},{6,4},{7,5},{8,10},{9,11},{10,... | collective-permute-start | bytes 442376 | tf_op jit(solution)/shard_map/while/body/eval_jaxpr/ppermute | solution.py:55
  27.4 4.0 %fusion.203 = f32[8,3,8,2,384]{4,2,3,1,0:T(8,128)S(1)} fusion(f32[8,3,8,2,384]{4,3,2,1,0:T(2,128)S(1)} %dot_general.108, f32[384]{0:T(512)} %get-tuple-element.802, f32[384]{0:T(512)} %get-tuple-element.803, f32[384]{0:T(512)S(1)} %get-tuple-element.804), kind=kOutput, calls=%fused_computation.46.clone.1 | convolution fusion | flops 679919616 | bytes 1184256 | tf_op jit(solution)/shard_map/while/body/eval_jaxpr/rz,zk->rk/dot_general | solution.py:47
  35.0 3.1 %convolution_bitcast_fusion.15 = f32[128,3,2,384]{0,3,1,2:T(8,128)} fusion(s32[12,8]{1,0:T(8,128)S(1)} %copy-done.14, f32[4,3,8,2,384]{4,2,3,1,0:T(8,128)S(1)} %copy.133, f32[8,3,8,2,384]{4,2,3,1,0:T(8,128)S(1)} %fusion.203), kind=kOutput, calls=%fused_computation.8.clone.1 | convolution fusion | flops 339984384 | bytes 2064768 | tf_op jit(solution)/shard_map/while/body/eval_jaxpr/sfq,fmqcz->smcz/dot_general | solution.py:47
  38.1 3.4 %copy.134 = f32[128,3,2,384]{3,2,1,0:T(2,128)} copy(f32[128,3,2,384]{0,3,1,2:T(8,128)} %convolution_bitcast_fusion.15) | data formatting | bytes 2359296 | tf_op jit(solution)/shard_map/while/body/eval_jaxpr/sfq,fmqcz->smcz/dot_general | solution.py:47
  41.5 12.0 %all-to-all-start = ((f32[128,3,2,384]{3,2,1,0:T(2,128)}), f32[128,3,2,384]{3,2,1,0:T(2,128)S(1)}, u32[]{:S(2)}, u32[]{:S(2)}) async-start(f32[128,3,2,384]{3,2,1,0:T(2,128)} %copy.134), calls=%async_computation | async-start | bytes 2359296 | tf_op jit(solution)/shard_map/while/body/eval_jaxpr/all_to_all | solution.py:129
  54.9 2.2 %cosine_multiply_fusion.8 = f32[16,16,384]{2,1,0:T(8,128)S(1)} fusion(f32[384]{0:T(512)} %get-tuple-element.800, f32[16,16]{1,0:T(8,128)} %get-tuple-element.801), kind=kLoop, calls=%fused_computation.56.clone.1 | loop fusion | flops 294912 | bytes 395776 | tf_op jit(solution)/shard_map/mul | solution.py:27
  57.0 28.1 %all-to-all-done = f32[128,3,2,384]{3,2,1,0:T(2,128)S(1)} async-done(((f32[128,3,2,384]{3,2,1,0:T(2,128)}), f32[128,3,2,384]{3,2,1,0:T(2,128)S(1)}, u32[]{:S(2)}, u32[]{:S(2)}) %all-to-all-start) | async-done | bytes 1179680 | tf_op jit(solution)/shard_map/while/body/eval_jaxpr/all_to_all | solution.py:129
  85.2 2.0 %fusion.204 = f32[12,3,8,2,384]{4,2,3,1,0:T(8,128)S(1)} fusion(f32[128,3,2,384]{3,2,1,0:T(2,128)S(1)} %all-to-all-done, pred[12,8]{1,0:T(8,128)(4,1)} %copy.135, s32[12,8]{1,0:T(8,128)S(1)} %get-tuple-element.809, f32[4,3,8,2,384]{4,2,3,1,0:T(8,128)} %copy-done.5, f32[8,3,8,2,384]{4,2,3,1,0:T(8,128)S(1)} %fusion.203), kind=kOutput, calls=%fused_computation.11.clone.1 | convolution fusion | flops 340426752 | bytes 2949600 | tf_op jit(solution)/shard_map/while/body/eval_jaxpr/fqs,smcz->fmqcz/dot_general | solution.py:47
  88.3 3.4 %fusion.209 = f32[2,3,16,384]{3,2,1,0:T(8,128)S(1)} fusion(f32[12,1,16,384]{3,2,1,0:T(8,128)S(1)} %get-tuple-element.731, f32[12,1,16,384]{3,2,1,0:T(8,128)S(1)} %get-tuple-element.732, f32[12,1,16,384]{3,2,1,0:T(8,128)S(1)} %get-tuple-element.733, f32[384]{0:T(512)} %get-tuple-element.802, f32[384]{0:T(512)} %get-tuple-element.803, ...), kind=kOutput, calls=%fused_computation.22.clone.1 | convolution fusion | flops 170754048 | bytes 1036800 | tf_op jit(solution)/shard_map/while/body/eval_jaxpr/fmxz,kz->xfmk/dot_general | solution.py:47
  94.7 1.6 collective-permute-start.5
  96.4 4.1 %fusion.206 = f32[2,192,384]{2,1,0:T(8,128)S(1)} fusion(f32[2,192,384]{2,1,0:T(8,128)S(1)} %bitcast.224, f32[384]{0:T(512)} %get-tuple-element.802, f32[384]{0:T(512)} %get-tuple-element.803, f32[384]{0:T(512)S(1)} %get-tuple-element.804), kind=kOutput, calls=%fused_computation.48.clone.1 | convolution fusion | flops 679919616 | bytes 1184256 | tf_op jit(solution)/shard_map/while/body/eval_jaxpr/rz,kz->rk/dot_general | solution.py:47
  103.4 3.6 %fusion.210 = (f32[16,16,384]{2,1,0:T(8,128)}, f32[16,16,384]{2,1,0:T(8,128)S(1)}) fusion(f32[16,16,384]{2,1,0:T(8,128)S(1)} %get-tuple-element.767, f32[16,16,384]{2,1,0:T(8,128)S(1)} %copy-done.8, f32[16,6]{0,1:T(8,128)S(1)} %get-tuple-element.798, f32[16,6,384]{2,0,1:T(8,128)S(1)} %convolution_bitcast_fusion.16, ...), kind=kOutput, calls=%fused_computation.229.clone.1 | convolution fusion | flops 7962624 | bytes 2116480 | tf_op jit(solution)/shard_map/while/body/eval_jaxpr/iyk,jy->ijk/dot_general | solution.py:47
  107.4 3.3 %fusion.202 = f32[16,6,384]{2,0,1:T(8,128)S(1)} fusion(f32[384]{0:T(512)} %get-tuple-element.802, f32[384]{0:T(512)} %get-tuple-element.803, f32[384]{0:T(512)S(1)} %get-tuple-element.804, f32[16,6,384]{2,1,0:T(8,128)S(1)} %convolution_bitcast_fusion.12), kind=kOutput, calls=%fused_computation.50.clone.1 | convolution fusion | flops 170311680 | bytes 299520 | tf_op jit(solution)/shard_map/while/body/eval_jaxpr/iyk,kz->iyz/dot_general | solution.py:47
  111.2 3.0 %collective-permute-start.1 = (f32[16,2304]{1,0:T(8,128)S(1)}, f32[16,2304]{1,0:T(8,128)}, u32[]{:S(2)}, u32[]{:S(2)}) collective-permute-start(f32[16,2304]{1,0:T(8,128)S(1)} %bitcast.231), channel_id=1, source_target_pairs={{0,2},{1,3},{2,0},{3,1},{4,6},{5,7},{6,4},{7,5},{8,10},{9,11},{10,... | collective-permute-start | bytes 442376 | tf_op jit(solution)/shard_map/while/body/eval_jaxpr/ppermute | solution.py:55
  114.2 1.6 collective-permute-start.2
  116.9 4.0 %fusion.203 = f32[8,3,8,2,384]{4,2,3,1,0:T(8,128)S(1)} fusion(f32[8,3,8,2,384]{4,3,2,1,0:T(2,128)S(1)} %dot_general.108, f32[384]{0:T(512)} %get-tuple-element.802, f32[384]{0:T(512)} %get-tuple-element.803, f32[384]{0:T(512)S(1)} %get-tuple-element.804), kind=kOutput, calls=%fused_computation.46.clone.1 | convolution fusion | flops 679919616 | bytes 1184256 | tf_op jit(solution)/shard_map/while/body/eval_jaxpr/rz,zk->rk/dot_general | solution.py:47
  124.5 3.1 %convolution_bitcast_fusion.15 = f32[128,3,2,384]{0,3,1,2:T(8,128)} fusion(s32[12,8]{1,0:T(8,128)S(1)} %copy-done.14, f32[4,3,8,2,384]{4,2,3,1,0:T(8,128)S(1)} %copy.133, f32[8,3,8,2,384]{4,2,3,1,0:T(8,128)S(1)} %fusion.203), kind=kOutput, calls=%fused_computation.8.clone.1 | convolution fusion | flops 339984384 | bytes 2064768 | tf_op jit(solution)/shard_map/while/body/eval_jaxpr/sfq,fmqcz->smcz/dot_general | solution.py:47
  127.6 3.4 %copy.134 = f32[128,3,2,384]{3,2,1,0:T(2,128)} copy(f32[128,3,2,384]{0,3,1,2:T(8,128)} %convolution_bitcast_fusion.15) | data formatting | bytes 2359296 | tf_op jit(solution)/shard_map/while/body/eval_jaxpr/sfq,fmqcz->smcz/dot_general | solution.py:47
  131.0 5.7 %all-to-all-start = ((f32[128,3,2,384]{3,2,1,0:T(2,128)}), f32[128,3,2,384]{3,2,1,0:T(2,128)S(1)}, u32[]{:S(2)}, u32[]{:S(2)}) async-start(f32[128,3,2,384]{3,2,1,0:T(2,128)} %copy.134), calls=%async_computation | async-start | bytes 2359296 | tf_op jit(solution)/shard_map/while/body/eval_jaxpr/all_to_all | solution.py:129
  138.0 2.2 %cosine_multiply_fusion.8 = f32[16,16,384]{2,1,0:T(8,128)S(1)} fusion(f32[384]{0:T(512)} %get-tuple-element.800, f32[16,16]{1,0:T(8,128)} %get-tuple-element.801), kind=kLoop, calls=%fused_computation.56.clone.1 | loop fusion | flops 294912 | bytes 395776 | tf_op jit(solution)/shard_map/mul | solution.py:27
  140.2 28.1 %all-to-all-done = f32[128,3,2,384]{3,2,1,0:T(2,128)S(1)} async-done(((f32[128,3,2,384]{3,2,1,0:T(2,128)}), f32[128,3,2,384]{3,2,1,0:T(2,128)S(1)}, u32[]{:S(2)}, u32[]{:S(2)}) %all-to-all-start) | async-done | bytes 1179680 | tf_op jit(solution)/shard_map/while/body/eval_jaxpr/all_to_all | solution.py:129
  168.3 2.0 %fusion.204 = f32[12,3,8,2,384]{4,2,3,1,0:T(8,128)S(1)} fusion(f32[128,3,2,384]{3,2,1,0:T(2,128)S(1)} %all-to-all-done, pred[12,8]{1,0:T(8,128)(4,1)} %copy.135, s32[12,8]{1,0:T(8,128)S(1)} %get-tuple-element.809, f32[4,3,8,2,384]{4,2,3,1,0:T(8,128)} %copy-done.5, f32[8,3,8,2,384]{4,2,3,1,0:T(8,128)S(1)} %fusion.203), kind=kOutput, calls=%fused_computation.11.clone.1 | convolution fusion | flops 340426752 | bytes 2949600 | tf_op jit(solution)/shard_map/while/body/eval_jaxpr/fqs,smcz->fmqcz/dot_general | solution.py:47
  171.5 3.4 %fusion.209 = f32[2,3,16,384]{3,2,1,0:T(8,128)S(1)} fusion(f32[12,1,16,384]{3,2,1,0:T(8,128)S(1)} %get-tuple-element.731, f32[12,1,16,384]{3,2,1,0:T(8,128)S(1)} %get-tuple-element.732, f32[12,1,16,384]{3,2,1,0:T(8,128)S(1)} %get-tuple-element.733, f32[384]{0:T(512)} %get-tuple-element.802, f32[384]{0:T(512)} %get-tuple-element.803, ...), kind=kOutput, calls=%fused_computation.22.clone.1 | convolution fusion | flops 170754048 | bytes 1036800 | tf_op jit(solution)/shard_map/while/body/eval_jaxpr/fmxz,kz->xfmk/dot_general | solution.py:47
  176.9 1.5 collective-permute-start.4
  179.7 4.1 %fusion.206 = f32[2,192,384]{2,1,0:T(8,128)S(1)} fusion(f32[2,192,384]{2,1,0:T(8,128)S(1)} %bitcast.224, f32[384]{0:T(512)} %get-tuple-element.802, f32[384]{0:T(512)} %get-tuple-element.803, f32[384]{0:T(512)S(1)} %get-tuple-element.804), kind=kOutput, calls=%fused_computation.48.clone.1 | convolution fusion | flops 679919616 | bytes 1184256 | tf_op jit(solution)/shard_map/while/body/eval_jaxpr/rz,kz->rk/dot_general | solution.py:47
  186.8 3.6 %fusion.210 = (f32[16,16,384]{2,1,0:T(8,128)}, f32[16,16,384]{2,1,0:T(8,128)S(1)}) fusion(f32[16,16,384]{2,1,0:T(8,128)S(1)} %get-tuple-element.767, f32[16,16,384]{2,1,0:T(8,128)S(1)} %copy-done.8, f32[16,6]{0,1:T(8,128)S(1)} %get-tuple-element.798, f32[16,6,384]{2,0,1:T(8,128)S(1)} %convolution_bitcast_fusion.16, ...), kind=kOutput, calls=%fused_computation.229.clone.1 | convolution fusion | flops 7962624 | bytes 2116480 | tf_op jit(solution)/shard_map/while/body/eval_jaxpr/iyk,jy->ijk/dot_general | solution.py:47
  190.4 2.2 %subtract_bitcast_fusion = f32[1,16,16,384]{3,2,1,0:T(8,128)} fusion(f32[16,16,384]{2,1,0:T(8,128)S(1)} %get-tuple-element.228, f32[16,16,384]{2,1,0:T(8,128)} %get-tuple-element.229), kind=kLoop, calls=%fused_computation.177 | loop fusion | flops 98304 | bytes 1179648 | tf_op jit(solution)/shard_map/broadcast_in_dim | solution.py:149
  (180 shorter events, 40.5 us)
Async XLA Ops:
  1.9 4.3 %copy-start.18 = (s32[6]{0:T(128)S(1)}, s32[6]{0:T(128)}, u32[]{:S(2)}) copy-start(s32[6]{0:T(128)} %constant.191) | copy-start | bytes 76
  3.2 3.7 %copy-start.12 = (f32[384]{0:T(512)}, f32[384]{0:T(512)S(1)}, u32[]{:S(2)}) copy-start(f32[384]{0:T(512)S(1)} %get-tuple-element.748) | copy-start | bytes 4612
  20.4 11.0 %collective-permute-start = (f32[16,2304]{1,0:T(8,128)S(1)}, f32[16,2304]{1,0:T(8,128)}, u32[]{:S(2)}, u32[]{:S(2)}) collective-permute-start(f32[16,2304]{1,0:T(8,128)S(1)} %bitcast.230), channel_id=1, source_target_pairs={{0,1},{1,2},{2,3},{3,0},{4,5},{5,6},{6,7},{7,4},{8,9},{9,10},{10,1... | collective-permute-start | bytes 442376 | tf_op jit(solution)/shard_map/while/body/eval_jaxpr/ppermute | solution.py:55
  22.1 10.3 %collective-permute-start.1 = (f32[16,2304]{1,0:T(8,128)S(1)}, f32[16,2304]{1,0:T(8,128)}, u32[]{:S(2)}, u32[]{:S(2)}) collective-permute-start(f32[16,2304]{1,0:T(8,128)S(1)} %bitcast.231), channel_id=1, source_target_pairs={{0,2},{1,3},{2,0},{3,1},{4,6},{5,7},{6,4},{7,5},{8,10},{9,11},{10,... | collective-permute-start | bytes 442376 | tf_op jit(solution)/shard_map/while/body/eval_jaxpr/ppermute | solution.py:55
  25.0 8.3 %collective-permute-start.2 = (f32[16,2304]{1,0:T(8,128)S(1)}, f32[16,2304]{1,0:T(8,128)}, u32[]{:S(2)}, u32[]{:S(2)}) collective-permute-start(f32[16,2304]{1,0:T(8,128)S(1)} %bitcast.232), channel_id=1, source_target_pairs={{0,3},{1,0},{2,1},{3,2},{4,7},{5,4},{6,5},{7,6},{8,11},{9,8},{10,9... | collective-permute-start | bytes 442376 | tf_op jit(solution)/shard_map/while/body/eval_jaxpr/ppermute | solution.py:55
  27.4 6.8 %copy-start.16 = (f32[64]{0:T(128)S(1)}, f32[64]{0:T(128)}, u32[]{:S(2)}) copy-start(f32[64]{0:T(128)} %get-tuple-element.806) | copy-start | bytes 772 | tf_op jit(solution)/shard_map/while
  27.4 6.8 %copy-start.17 = (f32[64]{0:T(128)S(1)}, f32[64]{0:T(128)}, u32[]{:S(2)}) copy-start(f32[64]{0:T(128)} %get-tuple-element.807) | copy-start | bytes 772 | tf_op jit(solution)/shard_map/while
  27.4 6.8 %copy-start.23 = (f32[16]{0:T(128)S(1)}, f32[16]{0:T(128)}, u32[]{:S(2)}) copy-start(f32[16]{0:T(128)} %get-tuple-element.805) | copy-start | bytes 196 | tf_op jit(solution)/shard_map/while
  35.0 6.5 %copy-start.5 = (f32[4,3,8,2,384]{4,2,3,1,0:T(8,128)}, f32[4,3,8,2,384]{4,2,3,1,0:T(8,128)S(1)}, u32[]{:S(2)}) copy-start(f32[4,3,8,2,384]{4,2,3,1,0:T(8,128)S(1)} %copy.133) | copy-start | bytes 884740 | tf_op jit(solution)/shard_map/while
  41.5 43.6 %all-to-all-start = ((f32[128,3,2,384]{3,2,1,0:T(2,128)}), f32[128,3,2,384]{3,2,1,0:T(2,128)S(1)}, u32[]{:S(2)}, u32[]{:S(2)}) async-start(f32[128,3,2,384]{3,2,1,0:T(2,128)} %copy.134), calls=%async_computation | async-start | bytes 2359296 | tf_op jit(solution)/shard_map/while/body/eval_jaxpr/all_to_all | solution.py:129
  91.8 4.6 %copy-start.6 = (f32[2,3,16,384]{3,2,1,0:T(8,128)}, f32[2,3,16,384]{3,2,1,0:T(8,128)S(1)}, u32[]{:S(2)}) copy-start(f32[2,3,16,384]{3,2,1,0:T(8,128)S(1)} %fusion.209) | copy-start | bytes 442372 | tf_op jit(solution)/shard_map/while
  92.6 9.6 %collective-permute-start.3 = (f32[16,2304]{1,0:T(8,128)}, f32[16,2304]{1,0:T(8,128)S(1)}, u32[]{:S(2)}, u32[]{:S(2)}) collective-permute-start(f32[16,2304]{1,0:T(8,128)} %reshape.570), channel_id=1, source_target_pairs={{0,1},{1,2},{2,3},{3,0},{4,5},{5,6},{6,7},{7,4},{8,9},{9,10},{10,1... | collective-permute-start | bytes 442376 | tf_op jit(solution)/shard_map/while/body/eval_jaxpr/ppermute | solution.py:55
  93.3 8.9 %collective-permute-start.4 = (f32[16,2304]{1,0:T(8,128)}, f32[16,2304]{1,0:T(8,128)S(1)}, u32[]{:S(2)}, u32[]{:S(2)}) collective-permute-start(f32[16,2304]{1,0:T(8,128)} %reshape.570), channel_id=1, source_target_pairs={{0,2},{1,3},{2,0},{3,1},{4,6},{5,7},{6,4},{7,5},{8,10},{9,11},{10,... | collective-permute-start | bytes 442376 | tf_op jit(solution)/shard_map/while/body/eval_jaxpr/ppermute | solution.py:55
  94.7 7.6 %collective-permute-start.5 = (f32[16,2304]{1,0:T(8,128)}, f32[16,2304]{1,0:T(8,128)S(1)}, u32[]{:S(2)}, u32[]{:S(2)}) collective-permute-start(f32[16,2304]{1,0:T(8,128)} %reshape.570), channel_id=1, source_target_pairs={{0,3},{1,0},{2,1},{3,2},{4,7},{5,4},{6,5},{7,6},{8,11},{9,8},{10,9... | collective-permute-start | bytes 442376 | tf_op jit(solution)/shard_map/while/body/eval_jaxpr/ppermute | solution.py:55
  96.4 5.0 %copy-start.2 = (f32[2,16,16,384]{3,2,1,0:T(8,128)S(1)}, f32[2,16,16,384]{3,2,1,0:T(8,128)}, u32[]{:S(2)}) copy-start(f32[2,16,16,384]{3,2,1,0:T(8,128)} %get-tuple-element.766) | copy-start | bytes 2359300 | tf_op jit(solution)/shard_map/while
  96.4 5.0 %copy-start.9 = (f32[16,16,384]{2,1,0:T(8,128)S(1)}, f32[16,16,384]{2,1,0:T(8,128)}, u32[]{:S(2)}) copy-start(f32[16,16,384]{2,1,0:T(8,128)} %get-tuple-element.795) | copy-start | bytes 1179652 | tf_op jit(solution)/shard_map/while
  102.1 4.9 %copy-start.3 = (f32[2,16,16,384]{3,2,1,0:T(8,128)}, f32[2,16,16,384]{3,2,1,0:T(8,128)S(1)}, u32[]{:S(2)}) copy-start(f32[2,16,16,384]{3,2,1,0:T(8,128)S(1)} %get-tuple-element.792) | copy-start | bytes 2359300 | tf_op jit(solution)/shard_map/while
  110.7 10.3 %collective-permute-start = (f32[16,2304]{1,0:T(8,128)S(1)}, f32[16,2304]{1,0:T(8,128)}, u32[]{:S(2)}, u32[]{:S(2)}) collective-permute-start(f32[16,2304]{1,0:T(8,128)S(1)} %bitcast.230), channel_id=1, source_target_pairs={{0,1},{1,2},{2,3},{3,0},{4,5},{5,6},{6,7},{7,4},{8,9},{9,10},{10,1... | collective-permute-start | bytes 442376 | tf_op jit(solution)/shard_map/while/body/eval_jaxpr/ppermute | solution.py:55
  111.2 10.7 %collective-permute-start.1 = (f32[16,2304]{1,0:T(8,128)S(1)}, f32[16,2304]{1,0:T(8,128)}, u32[]{:S(2)}, u32[]{:S(2)}) collective-permute-start(f32[16,2304]{1,0:T(8,128)S(1)} %bitcast.231), channel_id=1, source_target_pairs={{0,2},{1,3},{2,0},{3,1},{4,6},{5,7},{6,4},{7,5},{8,10},{9,11},{10,... | collective-permute-start | bytes 442376 | tf_op jit(solution)/shard_map/while/body/eval_jaxpr/ppermute | solution.py:55
  114.2 8.6 %collective-permute-start.2 = (f32[16,2304]{1,0:T(8,128)S(1)}, f32[16,2304]{1,0:T(8,128)}, u32[]{:S(2)}, u32[]{:S(2)}) collective-permute-start(f32[16,2304]{1,0:T(8,128)S(1)} %bitcast.232), channel_id=1, source_target_pairs={{0,3},{1,0},{2,1},{3,2},{4,7},{5,4},{6,5},{7,6},{8,11},{9,8},{10,9... | collective-permute-start | bytes 442376 | tf_op jit(solution)/shard_map/while/body/eval_jaxpr/ppermute | solution.py:55
  116.9 6.8 %copy-start.16 = (f32[64]{0:T(128)S(1)}, f32[64]{0:T(128)}, u32[]{:S(2)}) copy-start(f32[64]{0:T(128)} %get-tuple-element.806) | copy-start | bytes 772 | tf_op jit(solution)/shard_map/while
  116.9 6.8 %copy-start.17 = (f32[64]{0:T(128)S(1)}, f32[64]{0:T(128)}, u32[]{:S(2)}) copy-start(f32[64]{0:T(128)} %get-tuple-element.807) | copy-start | bytes 772 | tf_op jit(solution)/shard_map/while
  116.9 6.8 %copy-start.23 = (f32[16]{0:T(128)S(1)}, f32[16]{0:T(128)}, u32[]{:S(2)}) copy-start(f32[16]{0:T(128)} %get-tuple-element.805) | copy-start | bytes 196 | tf_op jit(solution)/shard_map/while
  124.5 6.5 %copy-start.5 = (f32[4,3,8,2,384]{4,2,3,1,0:T(8,128)}, f32[4,3,8,2,384]{4,2,3,1,0:T(8,128)S(1)}, u32[]{:S(2)}) copy-start(f32[4,3,8,2,384]{4,2,3,1,0:T(8,128)S(1)} %copy.133) | copy-start | bytes 884740 | tf_op jit(solution)/shard_map/while
  131.0 37.3 %all-to-all-start = ((f32[128,3,2,384]{3,2,1,0:T(2,128)}), f32[128,3,2,384]{3,2,1,0:T(2,128)S(1)}, u32[]{:S(2)}, u32[]{:S(2)}) async-start(f32[128,3,2,384]{3,2,1,0:T(2,128)} %copy.134), calls=%async_computation | async-start | bytes 2359296 | tf_op jit(solution)/shard_map/while/body/eval_jaxpr/all_to_all | solution.py:129
  174.9 4.8 %copy-start.6 = (f32[2,3,16,384]{3,2,1,0:T(8,128)}, f32[2,3,16,384]{3,2,1,0:T(8,128)S(1)}, u32[]{:S(2)}) copy-start(f32[2,3,16,384]{3,2,1,0:T(8,128)S(1)} %fusion.209) | copy-start | bytes 442372 | tf_op jit(solution)/shard_map/while
  175.8 9.8 %collective-permute-start.3 = (f32[16,2304]{1,0:T(8,128)}, f32[16,2304]{1,0:T(8,128)S(1)}, u32[]{:S(2)}, u32[]{:S(2)}) collective-permute-start(f32[16,2304]{1,0:T(8,128)} %reshape.570), channel_id=1, source_target_pairs={{0,1},{1,2},{2,3},{3,0},{4,5},{5,6},{6,7},{7,4},{8,9},{9,10},{10,1... | collective-permute-start | bytes 442376 | tf_op jit(solution)/shard_map/while/body/eval_jaxpr/ppermute | solution.py:55
  176.9 8.6 %collective-permute-start.4 = (f32[16,2304]{1,0:T(8,128)}, f32[16,2304]{1,0:T(8,128)S(1)}, u32[]{:S(2)}, u32[]{:S(2)}) collective-permute-start(f32[16,2304]{1,0:T(8,128)} %reshape.570), channel_id=1, source_target_pairs={{0,2},{1,3},{2,0},{3,1},{4,6},{5,7},{6,4},{7,5},{8,10},{9,11},{10,... | collective-permute-start | bytes 442376 | tf_op jit(solution)/shard_map/while/body/eval_jaxpr/ppermute | solution.py:55
  178.4 7.1 %collective-permute-start.5 = (f32[16,2304]{1,0:T(8,128)}, f32[16,2304]{1,0:T(8,128)S(1)}, u32[]{:S(2)}, u32[]{:S(2)}) collective-permute-start(f32[16,2304]{1,0:T(8,128)} %reshape.570), channel_id=1, source_target_pairs={{0,3},{1,0},{2,1},{3,2},{4,7},{5,4},{6,5},{7,6},{8,11},{9,8},{10,9... | collective-permute-start | bytes 442376 | tf_op jit(solution)/shard_map/while/body/eval_jaxpr/ppermute | solution.py:55
  179.7 5.0 %copy-start.2 = (f32[2,16,16,384]{3,2,1,0:T(8,128)S(1)}, f32[2,16,16,384]{3,2,1,0:T(8,128)}, u32[]{:S(2)}) copy-start(f32[2,16,16,384]{3,2,1,0:T(8,128)} %get-tuple-element.766) | copy-start | bytes 2359300 | tf_op jit(solution)/shard_map/while
  179.7 5.0 %copy-start.9 = (f32[16,16,384]{2,1,0:T(8,128)S(1)}, f32[16,16,384]{2,1,0:T(8,128)}, u32[]{:S(2)}) copy-start(f32[16,16,384]{2,1,0:T(8,128)} %get-tuple-element.795) | copy-start | bytes 1179652 | tf_op jit(solution)/shard_map/while
  185.5 4.9 %copy-start.3 = (f32[2,16,16,384]{3,2,1,0:T(8,128)}, f32[2,16,16,384]{3,2,1,0:T(8,128)S(1)}, u32[]{:S(2)}) copy-start(f32[2,16,16,384]{3,2,1,0:T(8,128)S(1)} %get-tuple-element.792) | copy-start | bytes 2359300 | tf_op jit(solution)/shard_map/while
  (21 other events, 27.9 us)

commit v3 on v0

--- a/solution.py
+++ b/solution.py
@@ -74,6 +74,7 @@
     gathered_rows = (slab_of[:, None] * edge + jnp.arange(edge)[None, :]).reshape(-1)
     plaza_cols = dct_rows_cols(gathered_rows, mine, plaza_len)
     plaza_rows = dct_rows_cols(mine, gathered_rows, plaza_len)
+    plaza_cols_t = plaza_cols.T
 
     small_cos, small_gain = update_factors(0, edge, edge, edge, height)
     plaza_cos, plaza_gain = update_factors(first_row, edge, plaza_len, edge, height)
@@ -116,8 +117,8 @@
         small_strips = small_strips.reshape(owned * 4, 3, edge, height)
         plaza_y = ein("iyk,kz->iyz", ein("ijk,jy->iyk", plaza_cur, side6), table_height)
         plaza_all = gather_slabs(plaza_y.reshape(edge, -1))
-        plaza_all = plaza_all.reshape(plaza_len, 6, height)
-        plaza_faces = ein("iyz,ix->yxz", plaza_all, plaza_cols)
+        plaza_faces = ein("xi,id->xd", plaza_cols_t, plaza_all)
+        plaza_faces = jnp.swapaxes(plaza_faces.reshape(edge, 6, height), 0, 1)
         plaza_strips = jnp.concatenate(
             [jnp.zeros_like(plaza_faces), plaza_faces], axis=0
         ).reshape(4, 3, edge, height)
@@ -133,8 +134,7 @@
         small_force = small_force.reshape(owned, edge, edge, height)
         plaza_layers = ein("fmxz,kz->xfmk", layers[owned * 4 + 2 :], table_height)
         plaza_gathered = gather_slabs(plaza_layers.reshape(edge, -1))
-        plaza_gathered = plaza_gathered.reshape(plaza_len, 6, height)
-        plaza_x = ein("xyk,ix->iyk", plaza_gathered, plaza_rows)
+        plaza_x = ein("ix,xd->id", plaza_rows, plaza_gathered).reshape(edge, 6, height)
         plaza_force = ein("iyk,jy->ijk", plaza_x, side6)
         small_next = small_cos * small_cur - small_old + small_gain * small_force
         plaza_next = plaza_cos * plaza_cur - plaza_old + plaza_gain * plaza_force

time: 172 us -> 172 us (level)
  local copies, waits for them, and re-layouts: 25 us -> 19 us
  matrix products: 39.6 us -> 43.5 us
  starting transfers between devices: 36.8 us -> 39.2 us
    concatenate x12 -> x0, local copies, waits for them, and re-layouts: 5.59 us -> none  [gather_slabs(): return jnp.concatenate(pieces, axis=0)]
    dot_general x24, matrix products: 39.6 us -> 43.5 us  [ein(): jnp.einsum(spec, a, b, precision=highest, preferred_element_type=jnp.floa...]
    ppermute x12, starting transfers between devices: 18 us -> 19.8 us  [gather_slabs(): pieces.append(lax.ppermute(block, 'split', perm))]
    while x36 -> x28, local copies, waits for them, and re-layouts: 4.23 us -> 3.47 us
  transfers between devices with their start and end apart: 14 -> 14, of which waited for: 5 -> 4; matrix products, arithmetic and copies ran while one was open for 16% -> 14% of each run, Pallas kernels for 0% -> 0%
where the time goes in v3:
time: 172 us
  waiting for transfers between devices  60 us (35%)
  matrix products  43.5 us (25%)
  starting transfers between devices  39.2 us (23%)
  local copies, waits for them, and re-layouts  19 us (11%)
  other arithmetic  8.66 us (5%)
    all_to_all x2, waiting for transfers between devices, time_step(): arrived = lax.all_to_all(outgoing, 'rect', 0, 0, tiled=True)  58.6 us
    dot_general x24, matrix products, ein(): jnp.einsum(spec, a, b, precision=highest, preferred_element_type=jnp.floa...  43.5 us
    ppermute x12, starting transfers between devices, gather_slabs(): pieces.append(lax.ppermute(block, 'split', perm))  19.8 us
    all_to_all x2, starting transfers between devices, time_step(): arrived = lax.all_to_all(outgoing, 'rect', 0, 0, tiled=True)  19.4 us
    dot_general x4, local copies, waits for them, and re-layouts, ein(): jnp.einsum(spec, a, b, precision=highest, preferred_element_type=jnp.floa...  4.59 us
    mul x2, other arithmetic, update_factors(): twice_cos = 2.0 * jnp.cos(phase_angle)  4.41 us
    unnamed x20, local copies, waits for them, and re-layouts  4.4 us
    while x28, local copies, waits for them, and re-layouts  3.47 us
  transfers between devices with their start and end apart: 14, of which 4 were waited for; matrix products, arithmetic and copies ran while one was open for 14% of the time, Pallas kernels for 0%

profile of v3, /device:TPU:2, one launch (start us, length us, event | category | flops | bytes accessed | tf_op | source)
XLA Modules:
  0.0 171.9 jit_solution(16356825559764774712)
XLA Ops:
  3.5 2.1 %fusion.124 = (f32[16,16,384]{2,1,0:T(8,128)}, f32[16,16,384]{2,1,0:T(8,128)}) fusion(f32[16,16]{1,0:T(8,128)S(1)} %get-tuple-element.746, f32[384]{0:T(512)S(1)} %get-tuple-element.736, f32[16,16]{1,0:T(8,128)S(1)} %get-tuple-element.737), kind=kLoop, calls=%fused_computation.155 | loop fusion | flops 7274496 | bytes 790016 | tf_op jit(solution)/shard_map/mul | solution.py:28
  9.5 161.4 %while.21 = (s32[]{:T(128)}, f32[2,16,16,384]{3,2,1,0:T(8,128)}, f32[2,16,16,384]{3,2,1,0:T(8,128)S(1)}, f32[16,16,384]{2,1,0:T(8,128)}, f32[16,16,384]{2,1,0:T(...) while((s32[]{:T(128)}, f32[2,16,16,384]{3,2,1,0:T(8,128)}, ...), condition=%wide.region_3.5_spmd.clone.clone.clone, body=%wide.region_2.4_spmd.clone.clone.clone.sunk | while | flops 3361830912 | bytes 54585700 | solution.py:143
  10.0 2.6 %convolution_bitcast_fusion.17 = f32[6,2,8,384]{3,2,1,0:T(8,128)S(1)} fusion(f32[384]{0:T(512)S(1)} %get-tuple-element.790, f32[384]{0:T(512)S(1)} %get-tuple-element.791, f32[384]{0:T(512)S(1)} %get-tuple-element.792, f32[16,6,384]{2,1,0:T(8,128)S(1)} %convolution_bitcast_fusion.16), kind=kOutput, calls=%fused_computation.22.clone.1 | convolution fusion | flops 170311680 | bytes 299520 | tf_op jit(solution)/shard_map/while/body/eval_jaxpr/iyk,kz->iyz/dot_general | solution.py:47
  12.6 1.7 collective-permute-start
  14.3 2.9 %collective-permute-start.1 = (f32[16,2304]{1,0:T(8,128)S(1)}, f32[16,2304]{1,0:T(8,128)}, u32[]{:S(2)}, u32[]{:S(2)}) collective-permute-start(f32[16,2304]{1,0:T(8,128)S(1)} %bitcast.174), channel_id=1, source_target_pairs={{0,2},{1,3},{2,0},{3,1},{4,6},{5,7},{6,4},{7,5},{8,10},{9,11},{10,... | collective-permute-start | bytes 442376 | tf_op jit(solution)/shard_map/while/body/eval_jaxpr/ppermute | solution.py:55
  19.6 3.3 %fusion.197 = f32[8,3,8,2,384]{4,2,3,1,0:T(8,128)S(1)} fusion(f32[8,3,8,2,384]{4,3,2,1,0:T(2,128)S(1)} %dot_general.113, f32[384]{0:T(512)S(1)} %get-tuple-element.790, f32[384]{0:T(512)S(1)} %get-tuple-element.791, f32[384]{0:T(512)S(1)} %get-tuple-element.792), kind=kOutput, calls=%fused_computation.47.clone.1 | convolution fusion | flops 679919616 | bytes 1184256 | tf_op jit(solution)/shard_map/while/body/eval_jaxpr/rz,zk->rk/dot_general | solution.py:47
  24.0 1.5 convolution_bitcast_fusion.18
  25.9 2.1 %convolution_bitcast_fusion.20 = f32[128,3,2,384]{0,3,1,2:T(8,128)S(1)} fusion(s32[12,8]{1,0:T(8,128)S(1)} %get-tuple-element.796, f32[4,3,8,2,384]{4,2,3,1,0:T(8,128)S(1)} %copy.87, f32[8,3,8,2,384]{4,2,3,1,0:T(8,128)S(1)} %fusion.197), kind=kOutput, calls=%fused_computation.10.clone.1 | convolution fusion | flops 339984384 | bytes 2064768 | tf_op jit(solution)/shard_map/while/body/eval_jaxpr/sfq,fmqcz->smcz/dot_general | solution.py:47
  27.9 1.9 %copy.88 = f32[128,3,2,384]{3,2,1,0:T(2,128)} copy(f32[128,3,2,384]{0,3,1,2:T(8,128)S(1)} %convolution_bitcast_fusion.20) | data formatting | bytes 2359296 | tf_op jit(solution)/shard_map/while/body/eval_jaxpr/sfq,fmqcz->smcz/dot_general | solution.py:47
  29.9 12.0 %all-to-all-start = ((f32[128,3,2,384]{3,2,1,0:T(2,128)}), f32[128,3,2,384]{3,2,1,0:T(2,128)S(1)}, u32[]{:S(2)}, u32[]{:S(2)}) async-start(f32[128,3,2,384]{3,2,1,0:T(2,128)} %copy.88), calls=%async_computation | async-start | bytes 2359296 | tf_op jit(solution)/shard_map/while/body/eval_jaxpr/all_to_all | solution.py:128
  42.0 2.2 %cosine_multiply_fusion.8 = f32[16,16,384]{2,1,0:T(8,128)} fusion(f32[384]{0:T(512)S(1)} %get-tuple-element.788, f32[16,16]{1,0:T(8,128)S(1)} %get-tuple-element.789), kind=kLoop, calls=%fused_computation.56.clone.1 | loop fusion | flops 294912 | bytes 395776 | tf_op jit(solution)/shard_map/mul | solution.py:27
  44.2 29.3 %all-to-all-done = f32[128,3,2,384]{3,2,1,0:T(2,128)S(1)} async-done(((f32[128,3,2,384]{3,2,1,0:T(2,128)}), f32[128,3,2,384]{3,2,1,0:T(2,128)S(1)}, u32[]{:S(2)}, u32[]{:S(2)}) %all-to-all-start) | async-done | bytes 1179680 | tf_op jit(solution)/shard_map/while/body/eval_jaxpr/all_to_all | solution.py:128
  75.7 2.8 %convolution_bitcast_fusion.21 = f32[16,2,3,384]{3,0,2,1:T(8,128)S(1)} fusion(f32[12,1,16,384]{3,2,1,0:T(8,128)S(1)} %get-tuple-element.723, f32[12,1,16,384]{3,2,1,0:T(8,128)S(1)} %get-tuple-element.724, f32[12,1,16,384]{3,2,1,0:T(8,128)S(1)} %get-tuple-element.725, f32[384]{0:T(512)S(1)} %get-tuple-element.790, f32[384]{0:T(512)S(1)} %get-tuple-element.791, ...), kind=kOutput, calls=%fused_computation.21.clone.1 | convolution fusion | flops 170754048 | bytes 1036800 | tf_op jit(solution)/shard_map/while/body/eval_jaxpr/fmxz,kz->xfmk/dot_general | solution.py:47
  80.5 2.4 %collective-permute-start.4 = (f32[16,2304]{1,0:T(8,128)}, f32[16,2304]{1,0:T(8,128)S(1)}, u32[]{:S(2)}, u32[]{:S(2)}) collective-permute-start(f32[16,2304]{1,0:T(8,128)} %reshape.559), channel_id=1, source_target_pairs={{0,2},{1,3},{2,0},{3,1},{4,6},{5,7},{6,4},{7,5},{8,10},{9,11},{10,... | collective-permute-start | bytes 442376 | tf_op jit(solution)/shard_map/while/body/eval_jaxpr/ppermute | solution.py:55
  82.9 1.6 collective-permute-start.5
  84.6 3.3 %fusion.200 = f32[2,192,384]{2,1,0:T(8,128)S(1)} fusion(f32[2,192,384]{2,1,0:T(8,128)S(1)} %bitcast.169, f32[384]{0:T(512)S(1)} %get-tuple-element.790, f32[384]{0:T(512)S(1)} %get-tuple-element.791, f32[384]{0:T(512)S(1)} %get-tuple-element.792), kind=kOutput, calls=%fused_computation.49.clone.1 | convolution fusion | flops 679919616 | bytes 1184256 | tf_op jit(solution)/shard_map/while/body/eval_jaxpr/rz,kz->rk/dot_general | solution.py:47
  90.0 1.4 convolution_bitcast_fusion.22
  91.5 1.9 %fusion.202 = f32[16,16,384]{2,1,0:T(8,128)S(1)} fusion(f32[16,16,384]{2,1,0:T(8,128)S(1)} %copy-done.6, f32[16,6,384]{2,1,0:T(8,128)S(1)} %reshape.560, f32[16,16,384]{2,1,0:T(8,128)S(1)} %copy-done.7, f32[16,16,384]{2,1,0:T(8,128)S(1)} %get-tuple-element.756, f32[16,16]{1,0:T(8,128)S(1)} %get-tuple-element.798, f32[384]{0:T(512)S(1)} %get-tuple-element.788, ...), kind=kOutput, calls=%fused_computation.17.clone.1 | convolution fusion | flops 7766016 | bytes 1723264 | tf_op jit(solution)/shard_map/while/body/eval_jaxpr/iyk,jy->ijk/dot_general | solution.py:47
  94.5 2.6 %convolution_bitcast_fusion.17 = f32[6,2,8,384]{3,2,1,0:T(8,128)S(1)} fusion(f32[384]{0:T(512)S(1)} %get-tuple-element.790, f32[384]{0:T(512)S(1)} %get-tuple-element.791, f32[384]{0:T(512)S(1)} %get-tuple-element.792, f32[16,6,384]{2,1,0:T(8,128)S(1)} %convolution_bitcast_fusion.16), kind=kOutput, calls=%fused_computation.22.clone.1 | convolution fusion | flops 170311680 | bytes 299520 | tf_op jit(solution)/shard_map/while/body/eval_jaxpr/iyk,kz->iyz/dot_general | solution.py:47
  97.8 2.4 %collective-permute-start.1 = (f32[16,2304]{1,0:T(8,128)S(1)}, f32[16,2304]{1,0:T(8,128)}, u32[]{:S(2)}, u32[]{:S(2)}) collective-permute-start(f32[16,2304]{1,0:T(8,128)S(1)} %bitcast.174), channel_id=1, source_target_pairs={{0,2},{1,3},{2,0},{3,1},{4,6},{5,7},{6,4},{7,5},{8,10},{9,11},{10,... | collective-permute-start | bytes 442376 | tf_op jit(solution)/shard_map/while/body/eval_jaxpr/ppermute | solution.py:55
  102.4 3.3 %fusion.197 = f32[8,3,8,2,384]{4,2,3,1,0:T(8,128)S(1)} fusion(f32[8,3,8,2,384]{4,3,2,1,0:T(2,128)S(1)} %dot_general.113, f32[384]{0:T(512)S(1)} %get-tuple-element.790, f32[384]{0:T(512)S(1)} %get-tuple-element.791, f32[384]{0:T(512)S(1)} %get-tuple-element.792), kind=kOutput, calls=%fused_computation.47.clone.1 | convolution fusion | flops 679919616 | bytes 1184256 | tf_op jit(solution)/shard_map/while/body/eval_jaxpr/rz,zk->rk/dot_general | solution.py:47
  106.1 1.5 convolution_bitcast_fusion.18
  107.9 2.1 %convolution_bitcast_fusion.20 = f32[128,3,2,384]{0,3,1,2:T(8,128)S(1)} fusion(s32[12,8]{1,0:T(8,128)S(1)} %get-tuple-element.796, f32[4,3,8,2,384]{4,2,3,1,0:T(8,128)S(1)} %copy.87, f32[8,3,8,2,384]{4,2,3,1,0:T(8,128)S(1)} %fusion.197), kind=kOutput, calls=%fused_computation.10.clone.1 | convolution fusion | flops 339984384 | bytes 2064768 | tf_op jit(solution)/shard_map/while/body/eval_jaxpr/sfq,fmqcz->smcz/dot_general | solution.py:47
  110.0 1.9 %copy.88 = f32[128,3,2,384]{3,2,1,0:T(2,128)} copy(f32[128,3,2,384]{0,3,1,2:T(8,128)S(1)} %convolution_bitcast_fusion.20) | data formatting | bytes 2359296 | tf_op jit(solution)/shard_map/while/body/eval_jaxpr/sfq,fmqcz->smcz/dot_general | solution.py:47
  111.9 7.4 %all-to-all-start = ((f32[128,3,2,384]{3,2,1,0:T(2,128)}), f32[128,3,2,384]{3,2,1,0:T(2,128)S(1)}, u32[]{:S(2)}, u32[]{:S(2)}) async-start(f32[128,3,2,384]{3,2,1,0:T(2,128)} %copy.88), calls=%async_computation | async-start | bytes 2359296 | tf_op jit(solution)/shard_map/while/body/eval_jaxpr/all_to_all | solution.py:128
  119.4 2.2 %cosine_multiply_fusion.8 = f32[16,16,384]{2,1,0:T(8,128)} fusion(f32[384]{0:T(512)S(1)} %get-tuple-element.788, f32[16,16]{1,0:T(8,128)S(1)} %get-tuple-element.789), kind=kLoop, calls=%fused_computation.56.clone.1 | loop fusion | flops 294912 | bytes 395776 | tf_op jit(solution)/shard_map/mul | solution.py:27
  121.6 29.3 %all-to-all-done = f32[128,3,2,384]{3,2,1,0:T(2,128)S(1)} async-done(((f32[128,3,2,384]{3,2,1,0:T(2,128)}), f32[128,3,2,384]{3,2,1,0:T(2,128)S(1)}, u32[]{:S(2)}, u32[]{:S(2)}) %all-to-all-start) | async-done | bytes 1179680 | tf_op jit(solution)/shard_map/while/body/eval_jaxpr/all_to_all | solution.py:128
  153.2 2.8 %convolution_bitcast_fusion.21 = f32[16,2,3,384]{3,0,2,1:T(8,128)S(1)} fusion(f32[12,1,16,384]{3,2,1,0:T(8,128)S(1)} %get-tuple-element.723, f32[12,1,16,384]{3,2,1,0:T(8,128)S(1)} %get-tuple-element.724, f32[12,1,16,384]{3,2,1,0:T(8,128)S(1)} %get-tuple-element.725, f32[384]{0:T(512)S(1)} %get-tuple-element.790, f32[384]{0:T(512)S(1)} %get-tuple-element.791, ...), kind=kOutput, calls=%fused_computation.21.clone.1 | convolution fusion | flops 170754048 | bytes 1036800 | tf_op jit(solution)/shard_map/while/body/eval_jaxpr/fmxz,kz->xfmk/dot_general | solution.py:47
  157.9 2.5 %collective-permute-start.4 = (f32[16,2304]{1,0:T(8,128)}, f32[16,2304]{1,0:T(8,128)S(1)}, u32[]{:S(2)}, u32[]{:S(2)}) collective-permute-start(f32[16,2304]{1,0:T(8,128)} %reshape.559), channel_id=1, source_target_pairs={{0,2},{1,3},{2,0},{3,1},{4,6},{5,7},{6,4},{7,5},{8,10},{9,11},{10,... | collective-permute-start | bytes 442376 | tf_op jit(solution)/shard_map/while/body/eval_jaxpr/ppermute | solution.py:55
  161.3 3.3 %fusion.200 = f32[2,192,384]{2,1,0:T(8,128)S(1)} fusion(f32[2,192,384]{2,1,0:T(8,128)S(1)} %bitcast.169, f32[384]{0:T(512)S(1)} %get-tuple-element.790, f32[384]{0:T(512)S(1)} %get-tuple-element.791, f32[384]{0:T(512)S(1)} %get-tuple-element.792), kind=kOutput, calls=%fused_computation.49.clone.1 | convolution fusion | flops 679919616 | bytes 1184256 | tf_op jit(solution)/shard_map/while/body/eval_jaxpr/rz,kz->rk/dot_general | solution.py:47
  166.7 1.4 convolution_bitcast_fusion.22
  168.2 1.9 %fusion.202 = f32[16,16,384]{2,1,0:T(8,128)S(1)} fusion(f32[16,16,384]{2,1,0:T(8,128)S(1)} %copy-done.6, f32[16,6,384]{2,1,0:T(8,128)S(1)} %reshape.560, f32[16,16,384]{2,1,0:T(8,128)S(1)} %copy-done.7, f32[16,16,384]{2,1,0:T(8,128)S(1)} %get-tuple-element.756, f32[16,16]{1,0:T(8,128)S(1)} %get-tuple-element.798, f32[384]{0:T(512)S(1)} %get-tuple-element.788, ...), kind=kOutput, calls=%fused_computation.17.clone.1 | convolution fusion | flops 7766016 | bytes 1723264 | tf_op jit(solution)/shard_map/while/body/eval_jaxpr/iyk,jy->ijk/dot_general | solution.py:47
  (134 shorter events, 30.9 us)
Async XLA Ops:
  0.6 1.1 copy-start.9
  0.6 2.0 %copy-start.10 = (f32[1,16,16,384]{3,2,1,0:T(8,128)S(1)}, f32[1,16,16,384]{3,2,1,0:T(8,128)}, u32[]{:S(2)}) copy-start(f32[1,16,16,384]{3,2,1,0:T(8,128)} %param.12) | copy-start | bytes 1179652
  2.6 3.1 %copy-start.11 = (s32[6]{0:T(128)S(1)}, s32[6]{0:T(128)}, u32[]{:S(2)}) copy-start(s32[6]{0:T(128)} %constant.191) | copy-start | bytes 76
  6.5 0.7 copy-start.12
  6.5 3.0 %copy-start.1 = (f32[2,16,16,384]{3,2,1,0:T(8,128)S(1)}, f32[2,16,16,384]{3,2,1,0:T(8,128)}, u32[]{:S(2)}) copy-start(f32[2,16,16,384]{3,2,1,0:T(8,128)} %param.9) | copy-start | bytes 2359300
  6.5 3.0 %copy-start.3 = (f32[1,16,16,384]{3,2,1,0:T(8,128)S(1)}, f32[1,16,16,384]{3,2,1,0:T(8,128)}, u32[]{:S(2)}) copy-start(f32[1,16,16,384]{3,2,1,0:T(8,128)} %param.11) | copy-start | bytes 1179652
  12.6 10.3 %collective-permute-start = (f32[16,2304]{1,0:T(8,128)S(1)}, f32[16,2304]{1,0:T(8,128)S(1)}, u32[]{:S(2)}, u32[]{:S(2)}) collective-permute-start(f32[16,2304]{1,0:T(8,128)S(1)} %bitcast.173), channel_id=1, source_target_pairs={{0,1},{1,2},{2,3},{3,0},{4,5},{5,6},{6,7},{7,4},{8,9},{9,10},{10,1... | collective-permute-start | bytes 442376 | tf_op jit(solution)/shard_map/while/body/eval_jaxpr/ppermute | solution.py:55
  14.3 9.7 %collective-permute-start.1 = (f32[16,2304]{1,0:T(8,128)S(1)}, f32[16,2304]{1,0:T(8,128)}, u32[]{:S(2)}, u32[]{:S(2)}) collective-permute-start(f32[16,2304]{1,0:T(8,128)S(1)} %bitcast.174), channel_id=1, source_target_pairs={{0,2},{1,3},{2,0},{3,1},{4,6},{5,7},{6,4},{7,5},{8,10},{9,11},{10,... | collective-permute-start | bytes 442376 | tf_op jit(solution)/shard_map/while/body/eval_jaxpr/ppermute | solution.py:55
  17.2 6.8 %collective-permute-start.2 = (f32[16,2304]{1,0:T(8,128)S(1)}, f32[16,2304]{1,0:T(8,128)}, u32[]{:S(2)}, u32[]{:S(2)}) collective-permute-start(f32[16,2304]{1,0:T(8,128)S(1)} %bitcast.175), channel_id=1, source_target_pairs={{0,3},{1,0},{2,1},{3,2},{4,7},{5,4},{6,5},{7,6},{8,11},{9,8},{10,9... | collective-permute-start | bytes 442376 | tf_op jit(solution)/shard_map/while/body/eval_jaxpr/ppermute | solution.py:55
  29.9 43.6 %all-to-all-start = ((f32[128,3,2,384]{3,2,1,0:T(2,128)}), f32[128,3,2,384]{3,2,1,0:T(2,128)S(1)}, u32[]{:S(2)}, u32[]{:S(2)}) async-start(f32[128,3,2,384]{3,2,1,0:T(2,128)} %copy.88), calls=%async_computation | async-start | bytes 2359296 | tf_op jit(solution)/shard_map/while/body/eval_jaxpr/all_to_all | solution.py:128
  79.3 10.7 %collective-permute-start.3 = (f32[16,2304]{1,0:T(8,128)}, f32[16,2304]{1,0:T(8,128)S(1)}, u32[]{:S(2)}, u32[]{:S(2)}) collective-permute-start(f32[16,2304]{1,0:T(8,128)} %reshape.559), channel_id=1, source_target_pairs={{0,1},{1,2},{2,3},{3,0},{4,5},{5,6},{6,7},{7,4},{8,9},{9,10},{10,1... | collective-permute-start | bytes 442376 | tf_op jit(solution)/shard_map/while/body/eval_jaxpr/ppermute | solution.py:55
  80.5 9.4 %collective-permute-start.4 = (f32[16,2304]{1,0:T(8,128)}, f32[16,2304]{1,0:T(8,128)S(1)}, u32[]{:S(2)}, u32[]{:S(2)}) collective-permute-start(f32[16,2304]{1,0:T(8,128)} %reshape.559), channel_id=1, source_target_pairs={{0,2},{1,3},{2,0},{3,1},{4,6},{5,7},{6,4},{7,5},{8,10},{9,11},{10,... | collective-permute-start | bytes 442376 | tf_op jit(solution)/shard_map/while/body/eval_jaxpr/ppermute | solution.py:55
  82.9 7.1 %collective-permute-start.5 = (f32[16,2304]{1,0:T(8,128)}, f32[16,2304]{1,0:T(8,128)S(1)}, u32[]{:S(2)}, u32[]{:S(2)}) collective-permute-start(f32[16,2304]{1,0:T(8,128)} %reshape.559), channel_id=1, source_target_pairs={{0,3},{1,0},{2,1},{3,2},{4,7},{5,4},{6,5},{7,6},{8,11},{9,8},{10,9... | collective-permute-start | bytes 442376 | tf_op jit(solution)/shard_map/while/body/eval_jaxpr/ppermute | solution.py:55
  84.5 4.2 %copy-start.4 = (f32[16,16,384]{2,1,0:T(8,128)S(1)}, f32[16,16,384]{2,1,0:T(8,128)}, u32[]{:S(2)}) copy-start(f32[16,16,384]{2,1,0:T(8,128)} %cosine_multiply_fusion.8) | copy-start | bytes 1179652 | tf_op jit(solution)/shard_map/while
  84.5 4.2 %copy-start.5 = (f32[2,16,16,384]{3,2,1,0:T(8,128)S(1)}, f32[2,16,16,384]{3,2,1,0:T(8,128)}, u32[]{:S(2)}) copy-start(f32[2,16,16,384]{3,2,1,0:T(8,128)} %get-tuple-element.753) | copy-start | bytes 2359300 | tf_op jit(solution)/shard_map/while
  84.6 4.2 %copy-start.8 = (f32[16,16,384]{2,1,0:T(8,128)S(1)}, f32[16,16,384]{2,1,0:T(8,128)}, u32[]{:S(2)}) copy-start(f32[16,16,384]{2,1,0:T(8,128)} %get-tuple-element.783) | copy-start | bytes 1179652 | tf_op jit(solution)/shard_map/while
  89.9 1.6 copy-start.6
  89.9 1.6 copy-start.7
  97.1 8.6 %collective-permute-start = (f32[16,2304]{1,0:T(8,128)S(1)}, f32[16,2304]{1,0:T(8,128)S(1)}, u32[]{:S(2)}, u32[]{:S(2)}) collective-permute-start(f32[16,2304]{1,0:T(8,128)S(1)} %bitcast.173), channel_id=1, source_target_pairs={{0,1},{1,2},{2,3},{3,0},{4,5},{5,6},{6,7},{7,4},{8,9},{9,10},{10,1... | collective-permute-start | bytes 442376 | tf_op jit(solution)/shard_map/while/body/eval_jaxpr/ppermute | solution.py:55
  97.8 7.9 %collective-permute-start.1 = (f32[16,2304]{1,0:T(8,128)S(1)}, f32[16,2304]{1,0:T(8,128)}, u32[]{:S(2)}, u32[]{:S(2)}) collective-permute-start(f32[16,2304]{1,0:T(8,128)S(1)} %bitcast.174), channel_id=1, source_target_pairs={{0,2},{1,3},{2,0},{3,1},{4,6},{5,7},{6,4},{7,5},{8,10},{9,11},{10,... | collective-permute-start | bytes 442376 | tf_op jit(solution)/shard_map/while/body/eval_jaxpr/ppermute | solution.py:55
  100.2 5.9 %collective-permute-start.2 = (f32[16,2304]{1,0:T(8,128)S(1)}, f32[16,2304]{1,0:T(8,128)}, u32[]{:S(2)}, u32[]{:S(2)}) collective-permute-start(f32[16,2304]{1,0:T(8,128)S(1)} %bitcast.175), channel_id=1, source_target_pairs={{0,3},{1,0},{2,1},{3,2},{4,7},{5,4},{6,5},{7,6},{8,11},{9,8},{10,9... | collective-permute-start | bytes 442376 | tf_op jit(solution)/shard_map/while/body/eval_jaxpr/ppermute | solution.py:55
  111.9 39.0 %all-to-all-start = ((f32[128,3,2,384]{3,2,1,0:T(2,128)}), f32[128,3,2,384]{3,2,1,0:T(2,128)S(1)}, u32[]{:S(2)}, u32[]{:S(2)}) async-start(f32[128,3,2,384]{3,2,1,0:T(2,128)} %copy.88), calls=%async_computation | async-start | bytes 2359296 | tf_op jit(solution)/shard_map/while/body/eval_jaxpr/all_to_all | solution.py:128
  156.7 10.0 %collective-permute-start.3 = (f32[16,2304]{1,0:T(8,128)}, f32[16,2304]{1,0:T(8,128)S(1)}, u32[]{:S(2)}, u32[]{:S(2)}) collective-permute-start(f32[16,2304]{1,0:T(8,128)} %reshape.559), channel_id=1, source_target_pairs={{0,1},{1,2},{2,3},{3,0},{4,5},{5,6},{6,7},{7,4},{8,9},{9,10},{10,1... | collective-permute-start | bytes 442376 | tf_op jit(solution)/shard_map/while/body/eval_jaxpr/ppermute | solution.py:55
  157.9 8.8 %collective-permute-start.4 = (f32[16,2304]{1,0:T(8,128)}, f32[16,2304]{1,0:T(8,128)S(1)}, u32[]{:S(2)}, u32[]{:S(2)}) collective-permute-start(f32[16,2304]{1,0:T(8,128)} %reshape.559), channel_id=1, source_target_pairs={{0,2},{1,3},{2,0},{3,1},{4,6},{5,7},{6,4},{7,5},{8,10},{9,11},{10,... | collective-permute-start | bytes 442376 | tf_op jit(solution)/shard_map/while/body/eval_jaxpr/ppermute | solution.py:55
  160.4 6.4 %collective-permute-start.5 = (f32[16,2304]{1,0:T(8,128)}, f32[16,2304]{1,0:T(8,128)S(1)}, u32[]{:S(2)}, u32[]{:S(2)}) collective-permute-start(f32[16,2304]{1,0:T(8,128)} %reshape.559), channel_id=1, source_target_pairs={{0,3},{1,0},{2,1},{3,2},{4,7},{5,4},{6,5},{7,6},{8,11},{9,8},{10,9... | collective-permute-start | bytes 442376 | tf_op jit(solution)/shard_map/while/body/eval_jaxpr/ppermute | solution.py:55
  161.3 4.2 %copy-start.4 = (f32[16,16,384]{2,1,0:T(8,128)S(1)}, f32[16,16,384]{2,1,0:T(8,128)}, u32[]{:S(2)}) copy-start(f32[16,16,384]{2,1,0:T(8,128)} %cosine_multiply_fusion.8) | copy-start | bytes 1179652 | tf_op jit(solution)/shard_map/while
  161.3 4.2 %copy-start.5 = (f32[2,16,16,384]{3,2,1,0:T(8,128)S(1)}, f32[2,16,16,384]{3,2,1,0:T(8,128)}, u32[]{:S(2)}) copy-start(f32[2,16,16,384]{3,2,1,0:T(8,128)} %get-tuple-element.753) | copy-start | bytes 2359300 | tf_op jit(solution)/shard_map/while
  161.3 4.2 %copy-start.8 = (f32[16,16,384]{2,1,0:T(8,128)S(1)}, f32[16,16,384]{2,1,0:T(8,128)}, u32[]{:S(2)}) copy-start(f32[16,16,384]{2,1,0:T(8,128)} %get-tuple-element.783) | copy-start | bytes 1179652 | tf_op jit(solution)/shard_map/while
  166.6 1.6 copy-start.6
  166.6 1.6 copy-start.7
  170.9 0.9 copy-start
  170.9 1.0 copy-start.2
